TPU v7x, 512 devices: a whole 4x8x8 slice. The times are simulated.
512 devices in a mesh: blk: 64 (over y, z_lo, core), head: 8 (over z_hi, x).
Axes of the slice: x: 4, y: 8, z: 8 (z_hi: 2, z_lo: 4; z = z_hi * 4 + z_lo), core: 2. Of those that a mesh axis runs over, the one named last changes fastest.
Arguments:
- query_rows: bfloat16 [16384, 5120], P(('blk', 'head')), may hold values from -12 to 12
- key_rows: bfloat16 [16384, 1024], P(('blk', 'head')), may hold values from -6 to 6
- value_rows: bfloat16 [16384, 1024], P(('blk', 'head')), may hold values from -6 to 6
- out_grads: bfloat16 [16384, 5120], P(('blk', 'head')), may hold values from -1.75 to 1.75
- lengths: int32 [128], replicated, may hold values from 1 to 128, as said below
- ancestors: int32 [128, 5], replicated, may hold values from -1 to 126, as said below
Outputs:
- query_grads: bfloat16 [16384, 5120], P(('blk', 'head'))
- key_grads: bfloat16 [16384, 1024], P(('blk', 'head'))
- value_grads: bfloat16 [16384, 1024], P(('blk', 'head'))
Inputs may be any that keep to these rules, and one draw needn't show every extreme that they name: `ancestors`: row t lists, in increasing order and followed by -1 entries, the tiles above tile t in the trie other than the 1 prompt tiles, which form a chain above every other tile. Every listed tile is a non-prompt tile below t that lies on the device of tile t or on one of the 2 devices before it; the last listed tile is the parent of t, and the row of a listed tile is a prefix of row t. Rows of prompt tiles are all -1. Some row has no -1 entry. On the devices before the last 3, the last tile of each device not a multiple of 3 has as parent the last tile of the device before, and the second-to-last tile of each device d >= 2 with d % 3 != 1 has as parent the second-to-last tile of the device before; those of the other devices have no non-prompt ancestor. lengths[t] slots of tile t hold tokens, the rest is padding; tile 0 is full.
All inputs are finite; a program needn't handle non-finite values.
Results may differ from a plain program's by a relative error of at most 0.0052.
Values may be sent and summed in bfloat16 or wider, within the bound.
No kernel may reach another device: no remote copies, remote signals or barrier semaphores. Data moves between devices by JAX's collectives and lax.ppermute only.
A program may use at most 64 MiB of HBM per device.

v0:
```python
import jax
import jax.numpy as jnp
from jax import lax
from jax.sharding import PartitionSpec as P

HD = 128
TILE = 128
SPAN_DEV = 2
PROMPT_TILES = 1
ANC = 5
KEYT = 7


def spread(value, axis, source):
    kept = jnp.where(lax.axis_index(axis) == source, value, 0).astype(value.dtype)
    return lax.psum(kept, axis)


def passed_along(block, axis, distance):
    devices = range(lax.axis_size(axis))
    route = [(i - distance, i) for i in devices if i - distance in devices]
    return lax.ppermute(block, axis, route)


def visible_mask(tile_id, tile_ids, listed, lengths):
    position = jnp.arange(TILE, dtype=jnp.int32)
    slot_ok = jnp.concatenate(
        [jnp.arange(PROMPT_TILES, dtype=jnp.int32) < tile_id, listed >= 0, jnp.ones((1,), bool)]
    )
    key_len = jnp.take(lengths, jnp.maximum(tile_ids, 0))
    key_ok = slot_ok[:, None] & (position[None, :] < key_len[:, None])
    own_slot = jnp.arange(KEYT) == KEYT - 1
    causal = position[None, None, :] <= position[:, None, None]
    allowed = key_ok[None, :, :] & (causal | ~own_slot[None, :, None])
    return allowed.reshape(TILE, KEYT * TILE)


def tile_backward(queries, grads_out, key_block, value_block, allowed, live_rows, scaling):
    scores = (
        jnp.einsum("igrd,jgd->grij", queries, key_block, preferred_element_type=jnp.float32)
        * scaling
    )
    scores = jnp.where(allowed, scores, -jnp.inf)
    row_max = jnp.max(scores, axis=-1, keepdims=True)
    log_total = row_max + jnp.log(jnp.sum(jnp.exp(scores - row_max), axis=-1, keepdims=True))
    weights = jnp.where(allowed & live_rows[:, None], jnp.exp(scores - log_total), 0.0)
    weight_grads = jnp.einsum(
        "igrd,jgd->grij", grads_out, value_block, preferred_element_type=jnp.float32
    )
    row_dot = jnp.sum(weights * weight_grads, axis=-1, keepdims=True)
    score_grads = (weights * (weight_grads - row_dot)).astype(jnp.bfloat16)
    weights_low = weights.astype(jnp.bfloat16)
    query_part = (
        jnp.einsum("grij,jgd->igrd", score_grads, key_block, preferred_element_type=jnp.float32)
        * scaling
    )
    key_part = jnp.einsum(
        "grij,igrd->jgd", score_grads, queries, preferred_element_type=jnp.float32
    )
    value_part = jnp.einsum(
        "grij,igrd->jgd", weights_low, grads_out, preferred_element_type=jnp.float32
    )
    return (query_part.astype(jnp.bfloat16), key_part, value_part)


def shards(query_rows, key_rows, value_rows, out_grads, lengths, ancestors):
    head_query, head_key, head_value, head_grad = (
        lax.all_to_all(query_rows, "head", split_axis=1, concat_axis=0, tiled=True),
        lax.all_to_all(key_rows, "head", split_axis=1, concat_axis=0, tiled=True),
        lax.all_to_all(value_rows, "head", split_axis=1, concat_axis=0, tiled=True),
        lax.all_to_all(out_grads, "head", split_axis=1, concat_axis=0, tiled=True),
    )
    row_count = head_query.shape[0]
    tiles_here = row_count // TILE
    kv_width = head_key.shape[1]
    kv_heads = kv_width // HD
    group_size = head_query.shape[1] // kv_width
    scaling = HD ** (-0.5)
    block_index = lax.axis_index("blk")
    first_tile = block_index * tiles_here
    window_first = (block_index - SPAN_DEV) * tiles_here
    window_slots = (SPAN_DEV + 1) * tiles_here
    own_states = jnp.concatenate(
        [
            head_key.reshape(tiles_here, TILE, kv_width),
            head_value.reshape(tiles_here, TILE, kv_width),
        ],
        axis=2,
    )
    my_lists = lax.dynamic_slice_in_dim(ancestors, first_tile, tiles_here, 0)
    prompt_ids = jnp.arange(PROMPT_TILES, dtype=jnp.int32)
    pieces = [spread(own_states[:PROMPT_TILES], "blk", 0)]
    for offset in range(SPAN_DEV, 0, -1):
        pieces.append(passed_along(own_states, "blk", offset))
    pieces.append(own_states)
    table = jnp.concatenate(pieces, axis=0)
    slot_index = jnp.arange(window_slots, dtype=jnp.int32)
    prompt_sum = jnp.zeros((PROMPT_TILES, TILE, 2 * kv_width), jnp.float32)
    near_sum = jnp.zeros((window_slots, TILE * 2 * kv_width), jnp.float32)
    query_parts = []
    for local in range(tiles_here):
        tile_id = first_tile + local
        listed = my_lists[local]
        tile_ids = jnp.concatenate([prompt_ids, listed, tile_id[None]])
        near_rows = jnp.where(listed >= 0, PROMPT_TILES + listed - window_first, 0)
        own_row = jnp.full((1,), PROMPT_TILES + SPAN_DEV * tiles_here + local, jnp.int32)
        table_rows = jnp.concatenate([prompt_ids, near_rows, own_row])
        chosen = jnp.take(table, table_rows, axis=0)
        key_block = chosen[:, :, :kv_width].reshape(KEYT * TILE, kv_heads, HD)
        value_block = chosen[:, :, kv_width:].reshape(KEYT * TILE, kv_heads, HD)
        allowed = visible_mask(tile_id, tile_ids, listed, lengths)
        live_rows = jnp.arange(TILE, dtype=jnp.int32) < lengths[tile_id]
        tile_query = head_query[local * TILE : (local + 1) * TILE].reshape(
            TILE, kv_heads, group_size, HD
        )
        tile_grad = head_grad[local * TILE : (local + 1) * TILE].reshape(
            TILE, kv_heads, group_size, HD
        )
        query_part, key_part, value_part = tile_backward(
            tile_query, tile_grad, key_block, value_block, allowed, live_rows, scaling
        )
        query_parts.append(query_part.reshape(TILE, group_size * kv_width))
        tile_terms = jnp.concatenate(
            [key_part.reshape(KEYT, TILE, kv_width), value_part.reshape(KEYT, TILE, kv_width)],
            axis=2,
        )
        prompt_sum = prompt_sum + tile_terms[:PROMPT_TILES]
        window_ids = jnp.concatenate(
            [listed - window_first, jnp.full((1,), SPAN_DEV * tiles_here + local, jnp.int32)]
        )
        usable = jnp.concatenate([listed >= 0, jnp.ones((1,), bool)])
        placing = ((window_ids[:, None] == slot_index[None, :]) & usable[:, None]).astype(
            jnp.float32
        )
        near_sum = near_sum + jnp.einsum(
            "sw,sx->wx",
            placing,
            tile_terms[PROMPT_TILES:].reshape(ANC + 1, TILE * 2 * kv_width),
            precision=lax.Precision.HIGHEST,
        )
    root_total = lax.psum(prompt_sum, "blk")
    near_parts = near_sum.reshape(SPAN_DEV + 1, tiles_here, TILE, 2 * kv_width)
    total = near_parts[SPAN_DEV]
    for offset in range(1, SPAN_DEV + 1):
        total = total + passed_along(near_parts[SPAN_DEV - offset], "blk", -offset)
    total = total.at[:PROMPT_TILES].add(jnp.where(block_index == 0, root_total, 0.0))
    key_out = (total[:, :, :kv_width] * scaling).astype(jnp.bfloat16).reshape(row_count, kv_width)
    value_out = total[:, :, kv_width:].astype(jnp.bfloat16).reshape(row_count, kv_width)
    query_out = jnp.concatenate(query_parts, axis=0)
    query_grads, key_grads, value_grads = (
        lax.all_to_all(query_out, "head", split_axis=0, concat_axis=1, tiled=True),
        lax.all_to_all(key_out, "head", split_axis=0, concat_axis=1, tiled=True),
        lax.all_to_all(value_out, "head", split_axis=0, concat_axis=1, tiled=True),
    )
    return (query_grads, key_grads, value_grads)


def solution(mesh):
    placed = (
        P(("blk", "head"), None),
        P(("blk", "head"), None),
        P(("blk", "head"), None),
        P(("blk", "head"), None),
        P(),
        P(),
    )
    return jax.shard_map(
        shards,
        mesh=mesh,
        in_specs=placed,
        out_specs=(P(("blk", "head"), None), P(("blk", "head"), None), P(("blk", "head"), None)),
        check_vma=False,
    )
```

profile of v0, /device:TPU:1, one launch (start us, length us, event | category | flops | bytes accessed | tf_op | source)
XLA Modules:
  0.0 1097.9 jit_solution(1257224561000166744)
XLA Ops:
  7.2 0.8 copy-done
  8.0 0.6 copy_bitcast_fusion.7
  8.7 13.3 %all-to-all-start = ((bf16[32,8,128]{2,0,1:T(8,128)(2,1)}), bf16[32,8,128]{2,0,1:T(8,128)(2,1)S(1)}, u32[]{:S(2)}, u32[]{:S(2)}) async-start(bf16[32,8,128]{2,0,1:T(8,128)(2,1)} %copy_bitcast_fusion.7), calls=%async_computation | async-start | bytes 131072 | tf_op jit(solution)/shard_map/all_to_all | solution.py:69
  22.0 0.8 constant_dynamic-slice_fusion
  23.4 1.4 fusion.74
  24.7 1.3 gather_fusion.3
  26.2 1.3 gather_fusion.1
  27.6 1.5 copy_bitcast_fusion.6
  29.0 1.3 iota_compare_fusion.3
  31.1 8.7 all-to-all-start.1
  39.8 1.7 copy.149
  41.6 0.7 copy.148
  42.8 6.1 all-to-all-done.1
  48.9 3.4 all-to-all-start.2
  52.4 3.1 collective-permute-start
  55.5 6.3 collective-permute-start.1
  61.8 0.6 fusion.43
  62.5 467.7 %all-reduce.3.cloned.1.call-done = bf16[1,128,256]{2,1,0:T(8,128)(2,1)} async-done(((bf16[1,128,256]{2,1,0:T(8,128)(2,1)}), bf16[1,128,256]{2,1,0:T(8,128)(2,1)}) %all-reduce.3.cloned.1.call-update) | async-done | bytes 65552 | tf_op jit(solution)/shard_map/psum | solution.py:16
  530.2 0.9 maximum_maximum_fusion
  531.1 0.6 gather_fusion.2
  532.5 8.3 all-to-all-start.3
  541.5 9.7 all-to-all-done.3
  552.4 0.7 fusion.14
  553.1 0.9 fusion.3
  554.1 0.7 fusion.10
  557.9 0.7 fusion.12
  558.6 1.0 fusion
  559.6 0.7 fusion.11
  561.3 0.8 fusion.45
  562.1 0.8 convolution_add_fusion
  563.3 8.0 collective-permute-start.2
  571.2 1.3 collective-permute-start.3
  573.1 0.7 fusion.26
  573.8 7.4 collective-permute-done.3
  581.2 1.1 fusion.24
  582.3 463.6 %all-reduce.5.cloned.1.call-done = f32[1,128,256]{2,1,0:T(8,128)} async-done(((f32[1,128,256]{2,1,0:T(8,128)}), f32[1,128,256]{2,1,0:T(8,128)}) %all-reduce.5.cloned.1.call-update) | async-done | bytes 131088 | tf_op jit(solution)/shard_map/psum | solution.py:141
  1046.0 0.6 slice.174
  1046.6 8.5 all-to-all-start.6
  1055.1 0.6 fusion.25
  1055.8 8.5 all-to-all-done.6
  1064.2 3.4 all-to-all-start.5
  1067.6 0.8 pad_maximum_fusion
  1068.3 8.3 all-to-all-done.5
  1076.6 3.4 all-to-all-start.4
  1080.1 0.6 copy_bitcast_fusion.4
  1080.7 0.6 copy_bitcast_fusion.5
  1081.3 9.0 all-to-all-done.4
  1090.3 0.8 copy.107
  (70 shorter events, 9.7 us)
Async XLA Ops:
  7.2 0.8 copy-start
  8.0 33.6 %copy-start.1 = (bf16[32,5120]{1,0:T(8,128)(2,1)S(1)}, bf16[32,5120]{1,0:T(8,128)(2,1)}, u32[]{:S(2)}) copy-start(bf16[32,5120]{1,0:T(8,128)(2,1)} %param.15) | copy-start | bytes 983044
  8.7 22.4 %all-to-all-start = ((bf16[32,8,128]{2,0,1:T(8,128)(2,1)}), bf16[32,8,128]{2,0,1:T(8,128)(2,1)S(1)}, u32[]{:S(2)}, u32[]{:S(2)}) async-start(bf16[32,8,128]{2,0,1:T(8,128)(2,1)} %copy_bitcast_fusion.7), calls=%async_computation | async-start | bytes 131072 | tf_op jit(solution)/shard_map/all_to_all | solution.py:69
  31.1 17.8 %all-to-all-start.1 = ((bf16[32,8,128]{2,0,1:T(8,128)(2,1)}), bf16[32,8,128]{2,0,1:T(8,128)(2,1)S(1)}, u32[]{:S(2)}, u32[]{:S(2)}) async-start(bf16[32,8,128]{2,0,1:T(8,128)(2,1)} %copy_bitcast_fusion.6), calls=%async_computation.1 | async-start | bytes 131072 | tf_op jit(solution)/shard_map/all_to_all | solution.py:70
  48.9 483.6 %all-to-all-start.2 = ((bf16[32,8,640]{2,0,1:T(8,128)(2,1)}), bf16[32,8,640]{2,0,1:T(8,128)(2,1)S(1)}, u32[]{:S(2)}, u32[]{:S(2)}) async-start(bf16[32,8,640]{2,0,1:T(8,128)(2,1)} %bitcast.235), calls=%async_computation.2 | async-start | bytes 655360 | tf_op jit(solution)/shard_map/all_to_all | solution.py:68
  52.3 477.9 %all-reduce.3.cloned.1.call-start = ((), (), s32[]{:S(2)}) async-start(), calls=%async_computation.7 | async-start | bytes 131072 | tf_op jit(solution)/shard_map/psum | solution.py:16
  52.4 477.8 %collective-permute-start = (bf16[2,128,256]{2,1,0:T(8,128)(2,1)S(1)}, bf16[2,128,256]{2,1,0:T(8,128)(2,1)S(1)}, u32[]{:S(2)}, u32[]{:S(2)}) collective-permute-start(bf16[2,128,256]{2,1,0:T(8,128)(2,1)S(1)} %pad_maximum_fusion.1), channel_id=1, source_target_pairs={{0,16},{8,24},{16,32},{24,40},{32,48},{40,56},{48,64},{56,72},{64,... | collective-permute-start | bytes 393224 | tf_op jit(solution)/shard_map/ppermute | solution.py:22
  55.5 474.7 %collective-permute-start.1 = (bf16[2,128,256]{2,1,0:T(8,128)(2,1)S(1)}, bf16[2,128,256]{2,1,0:T(8,128)(2,1)S(1)}, u32[]{:S(2)}, u32[]{:S(2)}) collective-permute-start(bf16[2,128,256]{2,1,0:T(8,128)(2,1)S(1)} %pad_maximum_fusion.1), channel_id=1, source_target_pairs={{0,8},{8,16},{16,24},{24,32},{32,40},{40,48},{48,56},{56,64},{64,7... | collective-permute-start | bytes 393224 | tf_op jit(solution)/shard_map/ppermute | solution.py:22
  532.5 18.7 %all-to-all-start.3 = ((bf16[32,8,640]{2,0,1:T(8,128)(2,1)}), bf16[32,8,640]{2,0,1:T(8,128)(2,1)S(1)}, u32[]{:S(2)}, u32[]{:S(2)}) async-start(bf16[32,8,640]{2,0,1:T(8,128)(2,1)} %bitcast.234), calls=%async_computation.3 | async-start | bytes 655360 | tf_op jit(solution)/shard_map/all_to_all | solution.py:71
  540.8 505.1 %all-reduce.5.cloned.1.call-start = ((), (), s32[]{:S(2)}) async-start(), calls=%async_computation.8 | async-start | bytes 262144 | tf_op jit(solution)/shard_map/psum | solution.py:141
  563.3 10.5 collective-permute-start.2
  571.2 10.0 collective-permute-start.3
  1046.6 17.6 %all-to-all-start.6 = ((bf16[8,32,128]{2,1,0:T(8,128)(2,1)}), bf16[8,32,128]{2,1,0:T(8,128)(2,1)S(1)}, u32[]{:S(2)}, u32[]{:S(2)}) async-start(bf16[8,32,128]{2,1,0:T(8,128)(2,1)} %bitcast.69), calls=%async_computation.6 | async-start | bytes 131072 | tf_op jit(solution)/shard_map/all_to_all | solution.py:153
  1064.2 12.4 %all-to-all-start.5 = ((bf16[8,32,128]{2,1,0:T(8,128)(2,1)}), bf16[8,32,128]{2,1,0:T(8,128)(2,1)S(1)}, u32[]{:S(2)}, u32[]{:S(2)}) async-start(bf16[8,32,128]{2,1,0:T(8,128)(2,1)} %bitcast.67), calls=%async_computation.5 | async-start | bytes 131072 | tf_op jit(solution)/shard_map/all_to_all | solution.py:152
  1076.6 13.7 %all-to-all-start.4 = ((bf16[8,32,640]{2,1,0:T(8,128)(2,1)}), bf16[8,32,640]{2,1,0:T(8,128)(2,1)S(1)}, u32[]{:S(2)}, u32[]{:S(2)}) async-start(bf16[8,32,640]{2,1,0:T(8,128)(2,1)} %bitcast.43), calls=%async_computation.4 | async-start | bytes 655360 | tf_op jit(solution)/shard_map/all_to_all | solution.py:151
Sparse Core Ops, SparseCore 0:
  62.6 467.5 all-reduce.2
  573.9 471.9 all-reduce.4
where the time goes:
time: 1100 us
  waiting for transfers between devices  981 us (89%)
  starting transfers between devices  67.9 us (6%)
  local copies, waits for them, and re-layouts  17.1 us (2%)
  between operations  14.5 us (1%)
    psum x1, waiting for transfers between devices, spread(): return lax.psum(kept, axis)  468 us
    psum x1, waiting for transfers between devices, shards(): root_total = lax.psum(prompt_sum, 'blk')  464 us
  transfers between devices with their start and end apart: 13, of which 9 were waited for; matrix products, arithmetic and copies ran while one was open for 2% of the time, Pallas kernels for 0%

commit v1 on v0

--- a/solution.py
+++ b/solution.py
@@ -14,6 +14,45 @@
 def spread(value, axis, source):
     kept = jnp.where(lax.axis_index(axis) == source, value, 0).astype(value.dtype)
     return lax.psum(kept, axis)
+
+
+def tree_levels(size):
+    levels = []
+    stride = 1
+    for radix in (2, 4):
+        if size % (stride * radix) == 0:
+            levels.append((stride, radix))
+            stride *= radix
+    if size // stride > 1:
+        levels.append((stride, size // stride))
+    return levels
+
+
+def tree_spread(value, axis):
+    size = lax.axis_size(axis)
+    index = lax.axis_index(axis)
+    for stride, radix in tree_levels(size):
+        got = [
+            lax.ppermute(value, axis, [(j, j + k * stride) for j in range(stride)])
+            for k in range(1, radix)
+        ]
+        arrived = got[0]
+        for extra in got[1:]:
+            arrived = arrived + extra
+        value = jnp.where(index < stride, value, arrived)
+    return value
+
+
+def tree_total(value, axis):
+    size = lax.axis_size(axis)
+    for stride, radix in reversed(tree_levels(size)):
+        got = [
+            lax.ppermute(value, axis, [(j + k * stride, j) for j in range(stride)])
+            for k in range(1, radix)
+        ]
+        for extra in got:
+            value = value + extra
+    return value
 
 
 def passed_along(block, axis, distance):
@@ -89,7 +128,7 @@
     )
     my_lists = lax.dynamic_slice_in_dim(ancestors, first_tile, tiles_here, 0)
     prompt_ids = jnp.arange(PROMPT_TILES, dtype=jnp.int32)
-    pieces = [spread(own_states[:PROMPT_TILES], "blk", 0)]
+    pieces = [tree_spread(own_states[:PROMPT_TILES], "blk")]
     for offset in range(SPAN_DEV, 0, -1):
         pieces.append(passed_along(own_states, "blk", offset))
     pieces.append(own_states)
@@ -138,7 +177,7 @@
             tile_terms[PROMPT_TILES:].reshape(ANC + 1, TILE * 2 * kv_width),
             precision=lax.Precision.HIGHEST,
         )
-    root_total = lax.psum(prompt_sum, "blk")
+    root_total = tree_total(prompt_sum, "blk")
     near_parts = near_sum.reshape(SPAN_DEV + 1, tiles_here, TILE, 2 * kv_width)
     total = near_parts[SPAN_DEV]
     for offset in range(1, SPAN_DEV + 1):

time: 1100 us -> 195 us (0.18)
  waiting for transfers between devices: 981 us -> 64.9 us
  starting transfers between devices: 67.9 us -> 94.1 us
  between operations: 14.5 us -> 1.44 us
    psum x2 -> x0, waiting for transfers between devices: 931 us -> none  [the longest x1 468 us: spread(): return lax.psum(kept, axis)]
    ppermute x0 -> x22, starting transfers between devices: none -> 29.6 us  [the longest x11 15.4 us: tree_total(): lax.ppermute(value, axis, [(j + k * stride, j) for j in range(stride)])]
    ppermute x0 -> x22, waiting for transfers between devices: none -> 19.9 us  [the longest x11 13.2 us: tree_total(): lax.ppermute(value, axis, [(j + k * stride, j) for j in range(stride)])]
  transfers between devices with their start and end apart: 13 -> 33, of which waited for: 9 -> 14; matrix products, arithmetic and copies ran while one was open for 2% -> 11% of each run, Pallas kernels for 0% -> 0%
where the time goes in v1:
time: 195 us; the launch traced here: 192 us
  starting transfers between devices  94.1 us (48%)
  waiting for transfers between devices  64.9 us (33%)
  local copies, waits for them, and re-layouts  17.1 us (9%)
  matrix products  7.67 us (4%)
  other arithmetic  7.12 us (4%)
    ppermute x4, starting transfers between devices, passed_along(): return lax.ppermute(block, axis, route)  20.4 us
    ppermute x11, starting transfers between devices, tree_total(): lax.ppermute(value, axis, [(j + k * stride, j) for j in range(stride)])  15.4 us
    ppermute x11, starting transfers between devices, tree_spread(): lax.ppermute(value, axis, [(j, j + k * stride) for j in range(stride)])  14.2 us
    all_to_all x1, starting transfers between devices, shards(): lax.all_to_all(key_rows, 'head', split_axis=1, concat_axis=0, tiled=True)  13.3 us
    ppermute x11, waiting for transfers between devices, tree_total(): lax.ppermute(value, axis, [(j + k * stride, j) for j in range(stride)])  13.2 us
    all_to_all x1, waiting for transfers between devices, shards(): lax.all_to_all(out_grads, 'head', split_axis=1, concat_axis=0, tiled=True)  10.8 us
    all_to_all x1, waiting for transfers between devices, shards(): lax.all_to_all(query_out, 'head', split_axis=0, concat_axis=1, tiled=True)  8.91 us
    all_to_all x1, waiting for transfers between devices, shards(): lax.all_to_all(value_out, 'head', split_axis=0, concat_axis=1, tiled=True)  8.46 us
  transfers between devices with their start and end apart: 33, of which 14 were waited for; matrix products, arithmetic and copies ran while one was open for 11% of the time, Pallas kernels for 0%

profile of v1, /device:TPU:1, one launch (start us, length us, event | category | flops | bytes accessed | tf_op | source)
XLA Modules:
  0.0 192.3 jit_solution(10797315413564991389)
XLA Ops:
  2.1 13.3 %all-to-all-start = ((bf16[32,8,128]{2,0,1:T(8,128)(2,1)}), bf16[32,8,128]{2,0,1:T(8,128)(2,1)S(1)}, u32[]{:S(2)}, u32[]{:S(2)}) async-start(bf16[32,8,128]{2,0,1:T(8,128)(2,1)} %copy_bitcast_fusion.7), calls=%async_computation | async-start | bytes 131072 | tf_op jit(solution)/shard_map/all_to_all | solution.py:108
  16.7 1.4 fusion.73
  18.0 1.3 gather_fusion.3
  19.4 1.3 gather_fusion.1
  20.8 1.5 copy_bitcast_fusion.6
  24.5 8.4 %all-to-all-start.1 = ((bf16[32,8,128]{2,0,1:T(8,128)(2,1)}), bf16[32,8,128]{2,0,1:T(8,128)(2,1)S(1)}, u32[]{:S(2)}, u32[]{:S(2)}) async-start(bf16[32,8,128]{2,0,1:T(8,128)(2,1)} %copy_bitcast_fusion.6), calls=%async_computation.1 | async-start | bytes 131072 | tf_op jit(solution)/shard_map/all_to_all | solution.py:109
  33.0 1.7 copy.147
  36.0 6.1 %all-to-all-done.1 = bf16[32,8,128]{2,0,1:T(8,128)(2,1)S(1)} async-done(((bf16[32,8,128]{2,0,1:T(8,128)(2,1)}), bf16[32,8,128]{2,0,1:T(8,128)(2,1)S(1)}, u32[]{:S(2)}, u32[]{:S(2)}) %all-to-all-start.1) | async-done | bytes 65568 | tf_op jit(solution)/shard_map/all_to_all | solution.py:109
  42.1 3.4 %all-to-all-start.2 = ((bf16[32,8,640]{2,0,1:T(8,128)(2,1)}), bf16[32,8,640]{2,0,1:T(8,128)(2,1)S(1)}, u32[]{:S(2)}, u32[]{:S(2)}) async-start(bf16[32,8,640]{2,0,1:T(8,128)(2,1)} %bitcast.235), calls=%async_computation.2 | async-start | bytes 655360 | tf_op jit(solution)/shard_map/all_to_all | solution.py:107
  45.5 1.3 collective-permute-start
  46.9 3.3 %collective-permute-done = bf16[1,128,256]{2,1,0:T(8,128)(2,1)S(1)} collective-permute-done((bf16[1,128,256]{2,1,0:T(8,128)(2,1)S(1)}, bf16[1,128,256]{2,1,0:T(8,128)(2,1)S(1)}, u32[]{:S(2)}, u32[]{:S(2)}) %collective-permute-start) | collective-permute-done | bytes 65568 | tf_op jit(solution)/shard_map/ppermute | solution.py:36
  50.2 1.3 collective-permute-start.3
  51.5 1.3 collective-permute-start.2
  52.8 1.3 collective-permute-start.1
  54.9 2.7 %collective-permute-done.1 = bf16[1,128,256]{2,1,0:T(8,128)(2,1)S(1)} collective-permute-done((bf16[1,128,256]{2,1,0:T(8,128)(2,1)S(1)}, bf16[1,128,256]{2,1,0:T(8,128)(2,1)S(1)}, u32[]{:S(2)}, u32[]{:S(2)}) %collective-permute-start.1) | collective-permute-done | bytes 65568 | tf_op jit(solution)/shard_map/ppermute | solution.py:36
  57.6 1.3 collective-permute-start.10
  58.9 1.3 collective-permute-start.9
  61.6 1.3 collective-permute-start.7
  62.9 1.3 collective-permute-start.6
  64.2 1.3 collective-permute-start.5
  65.5 1.3 collective-permute-start.4
  66.9 4.3 %collective-permute-start.11 = (bf16[2,128,256]{2,1,0:T(8,128)(2,1)S(1)}, bf16[2,128,256]{2,1,0:T(8,128)(2,1)S(1)}, u32[]{:S(2)}, u32[]{:S(2)}) collective-permute-start(bf16[2,128,256]{2,1,0:T(8,128)(2,1)S(1)} %pad_maximum_fusion.1), channel_id=1, source_target_pairs={{0,16},{8,24},{16,32},{24,40},{32,48},{40,56},{48,64},{56,72},{64,... | collective-permute-start | bytes 393224 | tf_op jit(solution)/shard_map/ppermute | solution.py:61
  71.1 5.1 %collective-permute-start.12 = (bf16[2,128,256]{2,1,0:T(8,128)(2,1)S(1)}, bf16[2,128,256]{2,1,0:T(8,128)(2,1)S(1)}, u32[]{:S(2)}, u32[]{:S(2)}) collective-permute-start(bf16[2,128,256]{2,1,0:T(8,128)(2,1)S(1)} %pad_maximum_fusion.1), channel_id=1, source_target_pairs={{0,8},{8,16},{16,24},{24,32},{32,40},{40,48},{48,56},{56,64},{64,7... | collective-permute-start | bytes 393224 | tf_op jit(solution)/shard_map/ppermute | solution.py:61
  76.3 1.8 collective-permute-done.12
  79.6 6.9 %all-to-all-start.3 = ((bf16[32,8,640]{2,0,1:T(8,128)(2,1)}), bf16[32,8,640]{2,0,1:T(8,128)(2,1)S(1)}, u32[]{:S(2)}, u32[]{:S(2)}) async-start(bf16[32,8,640]{2,0,1:T(8,128)(2,1)} %bitcast.234), calls=%async_computation.3 | async-start | bytes 655360 | tf_op jit(solution)/shard_map/all_to_all | solution.py:110
  87.2 10.8 %all-to-all-done.3 = bf16[32,8,640]{2,0,1:T(8,128)(2,1)S(1)} async-done(((bf16[32,8,640]{2,0,1:T(8,128)(2,1)}), bf16[32,8,640]{2,0,1:T(8,128)(2,1)S(1)}, u32[]{:S(2)}, u32[]{:S(2)}) %all-to-all-start.3) | async-done | bytes 327712 | tf_op jit(solution)/shard_map/all_to_all | solution.py:110
  106.5 1.3 collective-permute-start.21
  107.8 1.3 collective-permute-start.20
  109.1 1.3 collective-permute-start.19
  110.4 1.5 collective-permute-start.18
  111.8 1.3 collective-permute-start.17
  116.0 1.3 collective-permute-start.16
  117.3 1.3 collective-permute-start.15
  119.1 9.8 %collective-permute-start.13 = (f32[2,128,256]{2,1,0:T(8,128)S(1)}, f32[2,128,256]{2,1,0:T(8,128)S(1)}, u32[]{:S(2)}, u32[]{:S(2)}) collective-permute-start(f32[2,128,256]{2,1,0:T(8,128)S(1)} %bitcast.270), channel_id=1, source_target_pairs={{8,0},{16,8},{24,16},{32,24},{40,32},{48,40},{56,48},{64,56},{72,6... | collective-permute-start | bytes 786440 | tf_op jit(solution)/shard_map/ppermute | solution.py:61
  128.9 1.3 collective-permute-start.14
  130.3 1.3 collective-permute-start.24
  131.6 1.3 collective-permute-start.23
  132.9 1.3 collective-permute-start.22
  134.9 3.0 %collective-permute-done.24 = f32[1,128,256]{2,1,0:T(8,128)S(1)} collective-permute-done((f32[1,128,256]{2,1,0:T(8,128)S(1)}, f32[1,128,256]{2,1,0:T(8,128)S(1)}, u32[]{:S(2)}, u32[]{:S(2)}) %collective-permute-start.24) | collective-permute-done | bytes 131104 | tf_op jit(solution)/shard_map/ppermute | solution.py:50
  137.9 5.3 %collective-permute-done.23 = f32[1,128,256]{2,1,0:T(8,128)S(1)} collective-permute-done((f32[1,128,256]{2,1,0:T(8,128)S(1)}, f32[1,128,256]{2,1,0:T(8,128)S(1)}, u32[]{:S(2)}, u32[]{:S(2)}) %collective-permute-start.23) | collective-permute-done | bytes 131104 | tf_op jit(solution)/shard_map/ppermute | solution.py:50
  143.2 4.0 %collective-permute-done.22 = f32[1,128,256]{2,1,0:T(8,128)S(1)} collective-permute-done((f32[1,128,256]{2,1,0:T(8,128)S(1)}, f32[1,128,256]{2,1,0:T(8,128)S(1)}, u32[]{:S(2)}, u32[]{:S(2)}) %collective-permute-start.22) | collective-permute-done | bytes 131104 | tf_op jit(solution)/shard_map/ppermute | solution.py:50
  147.3 2.3 %collective-permute-start.25 = (f32[1,128,256]{2,1,0:T(8,128)S(1)}, f32[1,128,256]{2,1,0:T(8,128)S(1)}, u32[]{:S(2)}, u32[]{:S(2)}) collective-permute-start(f32[1,128,256]{2,1,0:T(8,128)S(1)} %add_add_fusion), channel_id=1, source_target_pairs={{8,0},{9,1},{10,2},{11,3},{12,4},{13,5},{14,6},{15,7}} | collective-permute-start | bytes 393224 | tf_op jit(solution)/shard_map/ppermute | solution.py:50
  151.2 5.2 %all-to-all-start.6 = ((bf16[8,32,128]{2,1,0:T(8,128)(2,1)}), bf16[8,32,128]{2,1,0:T(8,128)(2,1)S(1)}, u32[]{:S(2)}, u32[]{:S(2)}) async-start(bf16[8,32,128]{2,1,0:T(8,128)(2,1)} %bitcast.69), calls=%async_computation.6 | async-start | bytes 131072 | tf_op jit(solution)/shard_map/all_to_all | solution.py:192
  157.1 8.5 %all-to-all-done.6 = bf16[8,32,128]{2,1,0:T(8,128)(2,1)S(1)} async-done(((bf16[8,32,128]{2,1,0:T(8,128)(2,1)}), bf16[8,32,128]{2,1,0:T(8,128)(2,1)S(1)}, u32[]{:S(2)}, u32[]{:S(2)}) %all-to-all-start.6) | async-done | bytes 65568 | tf_op jit(solution)/shard_map/all_to_all | solution.py:192
  165.5 3.4 %all-to-all-start.5 = ((bf16[8,32,128]{2,1,0:T(8,128)(2,1)}), bf16[8,32,128]{2,1,0:T(8,128)(2,1)S(1)}, u32[]{:S(2)}, u32[]{:S(2)}) async-start(bf16[8,32,128]{2,1,0:T(8,128)(2,1)} %bitcast.67), calls=%async_computation.5 | async-start | bytes 131072 | tf_op jit(solution)/shard_map/all_to_all | solution.py:191
  169.7 8.3 %all-to-all-done.5 = bf16[8,32,128]{2,1,0:T(8,128)(2,1)S(1)} async-done(((bf16[8,32,128]{2,1,0:T(8,128)(2,1)}), bf16[8,32,128]{2,1,0:T(8,128)(2,1)S(1)}, u32[]{:S(2)}, u32[]{:S(2)}) %all-to-all-start.5) | async-done | bytes 65568 | tf_op jit(solution)/shard_map/all_to_all | solution.py:191
  177.9 3.4 %all-to-all-start.4 = ((bf16[8,32,640]{2,1,0:T(8,128)(2,1)}), bf16[8,32,640]{2,1,0:T(8,128)(2,1)S(1)}, u32[]{:S(2)}, u32[]{:S(2)}) async-start(bf16[8,32,640]{2,1,0:T(8,128)(2,1)} %bitcast.43), calls=%async_computation.4 | async-start | bytes 655360 | tf_op jit(solution)/shard_map/all_to_all | solution.py:190
  182.6 8.9 %all-to-all-done.4 = bf16[8,32,640]{2,1,0:T(8,128)(2,1)S(1)} async-done(((bf16[8,32,640]{2,1,0:T(8,128)(2,1)}), bf16[8,32,640]{2,1,0:T(8,128)(2,1)S(1)}, u32[]{:S(2)}, u32[]{:S(2)}) %all-to-all-start.4) | async-done | bytes 327712 | tf_op jit(solution)/shard_map/all_to_all | solution.py:190
  (113 shorter events, 28.2 us)
Async XLA Ops:
  0.6 0.8 copy-start
  1.5 33.3 %copy-start.1 = (bf16[32,5120]{1,0:T(8,128)(2,1)S(1)}, bf16[32,5120]{1,0:T(8,128)(2,1)}, u32[]{:S(2)}) copy-start(bf16[32,5120]{1,0:T(8,128)(2,1)} %param.15) | copy-start | bytes 983044
  2.1 22.4 %all-to-all-start = ((bf16[32,8,128]{2,0,1:T(8,128)(2,1)}), bf16[32,8,128]{2,0,1:T(8,128)(2,1)S(1)}, u32[]{:S(2)}, u32[]{:S(2)}) async-start(bf16[32,8,128]{2,0,1:T(8,128)(2,1)} %copy_bitcast_fusion.7), calls=%async_computation | async-start | bytes 131072 | tf_op jit(solution)/shard_map/all_to_all | solution.py:108
  24.5 17.6 %all-to-all-start.1 = ((bf16[32,8,128]{2,0,1:T(8,128)(2,1)}), bf16[32,8,128]{2,0,1:T(8,128)(2,1)S(1)}, u32[]{:S(2)}, u32[]{:S(2)}) async-start(bf16[32,8,128]{2,0,1:T(8,128)(2,1)} %copy_bitcast_fusion.6), calls=%async_computation.1 | async-start | bytes 131072 | tf_op jit(solution)/shard_map/all_to_all | solution.py:109
  42.1 37.5 %all-to-all-start.2 = ((bf16[32,8,640]{2,0,1:T(8,128)(2,1)}), bf16[32,8,640]{2,0,1:T(8,128)(2,1)S(1)}, u32[]{:S(2)}, u32[]{:S(2)}) async-start(bf16[32,8,640]{2,0,1:T(8,128)(2,1)} %bitcast.235), calls=%async_computation.2 | async-start | bytes 655360 | tf_op jit(solution)/shard_map/all_to_all | solution.py:107
  45.5 4.7 %collective-permute-start = (bf16[1,128,256]{2,1,0:T(8,128)(2,1)S(1)}, bf16[1,128,256]{2,1,0:T(8,128)(2,1)S(1)}, u32[]{:S(2)}, u32[]{:S(2)}) collective-permute-start(bf16[1,128,256]{2,1,0:T(8,128)(2,1)S(1)} %fusion.42), channel_id=1, source_target_pairs={{0,8},{1,9},{2,10},{3,11},{4,12},{5,13},{6,14},{7,15}} | collective-permute-start | bytes 196616 | tf_op jit(solution)/shard_map/ppermute | solution.py:36
  50.2 4.0 %collective-permute-start.3 = (bf16[1,128,256]{2,1,0:T(8,128)(2,1)S(1)}, bf16[1,128,256]{2,1,0:T(8,128)(2,1)S(1)}, u32[]{:S(2)}, u32[]{:S(2)}) collective-permute-start(bf16[1,128,256]{2,1,0:T(8,128)(2,1)S(1)} %broadcast_select_fusion.2), channel_id=1, source_target_pairs={{0,48},{8,56},{1,49},{9,57},{2,50},{10,58},{3,51},{11,59},{4,52},{... | collective-permute-start | bytes 196616 | tf_op jit(solution)/shard_map/ppermute | solution.py:36
  51.5 3.4 %collective-permute-start.2 = (bf16[1,128,256]{2,1,0:T(8,128)(2,1)S(1)}, bf16[1,128,256]{2,1,0:T(8,128)(2,1)S(1)}, u32[]{:S(2)}, u32[]{:S(2)}) collective-permute-start(bf16[1,128,256]{2,1,0:T(8,128)(2,1)S(1)} %broadcast_select_fusion.2), channel_id=1, source_target_pairs={{0,32},{8,40},{1,33},{9,41},{2,34},{10,42},{3,35},{11,43},{4,36},{... | collective-permute-start | bytes 196616 | tf_op jit(solution)/shard_map/ppermute | solution.py:36
  52.8 4.8 %collective-permute-start.1 = (bf16[1,128,256]{2,1,0:T(8,128)(2,1)S(1)}, bf16[1,128,256]{2,1,0:T(8,128)(2,1)S(1)}, u32[]{:S(2)}, u32[]{:S(2)}) collective-permute-start(bf16[1,128,256]{2,1,0:T(8,128)(2,1)S(1)} %broadcast_select_fusion.2), channel_id=1, source_target_pairs={{0,16},{8,24},{1,17},{9,25},{2,18},{10,26},{3,19},{11,27},{4,20},{... | collective-permute-start | bytes 196616 | tf_op jit(solution)/shard_map/ppermute | solution.py:36
  57.6 6.6 %collective-permute-start.10 = (bf16[1,128,256]{2,1,0:T(8,128)(2,1)S(1)}, bf16[1,128,256]{2,1,0:T(8,128)(2,1)S(1)}, u32[]{:S(2)}, u32[]{:S(2)}) collective-permute-start(bf16[1,128,256]{2,1,0:T(8,128)(2,1)S(1)} %add_select_fusion.1), channel_id=1, source_target_pairs={{0,448},{8,456},{16,464},{24,472},{32,480},{40,488},{48,496},{56,5... | collective-permute-start | bytes 196616 | tf_op jit(solution)/shard_map/ppermute | solution.py:36
  58.9 6.6 %collective-permute-start.9 = (bf16[1,128,256]{2,1,0:T(8,128)(2,1)S(1)}, bf16[1,128,256]{2,1,0:T(8,128)(2,1)S(1)}, u32[]{:S(2)}, u32[]{:S(2)}) collective-permute-start(bf16[1,128,256]{2,1,0:T(8,128)(2,1)S(1)} %add_select_fusion.1), channel_id=1, source_target_pairs={{0,384},{8,392},{16,400},{24,408},{32,416},{40,424},{48,432},{56,4... | collective-permute-start | bytes 196616 | tf_op jit(solution)/shard_map/ppermute | solution.py:36
  60.3 6.5 %collective-permute-start.8 = (bf16[1,128,256]{2,1,0:T(8,128)(2,1)S(1)}, bf16[1,128,256]{2,1,0:T(8,128)(2,1)S(1)}, u32[]{:S(2)}, u32[]{:S(2)}) collective-permute-start(bf16[1,128,256]{2,1,0:T(8,128)(2,1)S(1)} %add_select_fusion.1), channel_id=1, source_target_pairs={{0,320},{8,328},{16,336},{24,344},{32,352},{40,360},{48,368},{56,3... | collective-permute-start | bytes 196616 | tf_op jit(solution)/shard_map/ppermute | solution.py:36
  61.6 9.5 %collective-permute-start.7 = (bf16[1,128,256]{2,1,0:T(8,128)(2,1)S(1)}, bf16[1,128,256]{2,1,0:T(8,128)(2,1)S(1)}, u32[]{:S(2)}, u32[]{:S(2)}) collective-permute-start(bf16[1,128,256]{2,1,0:T(8,128)(2,1)S(1)} %add_select_fusion.1), channel_id=1, source_target_pairs={{0,256},{8,264},{16,272},{24,280},{32,288},{40,296},{48,304},{56,3... | collective-permute-start | bytes 196616 | tf_op jit(solution)/shard_map/ppermute | solution.py:36
  62.9 13.3 %collective-permute-start.6 = (bf16[1,128,256]{2,1,0:T(8,128)(2,1)S(1)}, bf16[1,128,256]{2,1,0:T(8,128)(2,1)S(1)}, u32[]{:S(2)}, u32[]{:S(2)}) collective-permute-start(bf16[1,128,256]{2,1,0:T(8,128)(2,1)S(1)} %add_select_fusion.1), channel_id=1, source_target_pairs={{0,192},{8,200},{16,208},{24,216},{32,224},{40,232},{48,240},{56,2... | collective-permute-start | bytes 196616 | tf_op jit(solution)/shard_map/ppermute | solution.py:36
  64.2 12.0 %collective-permute-start.5 = (bf16[1,128,256]{2,1,0:T(8,128)(2,1)S(1)}, bf16[1,128,256]{2,1,0:T(8,128)(2,1)S(1)}, u32[]{:S(2)}, u32[]{:S(2)}) collective-permute-start(bf16[1,128,256]{2,1,0:T(8,128)(2,1)S(1)} %add_select_fusion.1), channel_id=1, source_target_pairs={{0,128},{8,136},{16,144},{24,152},{32,160},{40,168},{48,176},{56,1... | collective-permute-start | bytes 196616 | tf_op jit(solution)/shard_map/ppermute | solution.py:36
  65.5 10.7 %collective-permute-start.4 = (bf16[1,128,256]{2,1,0:T(8,128)(2,1)S(1)}, bf16[1,128,256]{2,1,0:T(8,128)(2,1)S(1)}, u32[]{:S(2)}, u32[]{:S(2)}) collective-permute-start(bf16[1,128,256]{2,1,0:T(8,128)(2,1)S(1)} %add_select_fusion.1), channel_id=1, source_target_pairs={{0,64},{8,72},{16,80},{24,88},{32,96},{40,104},{48,112},{56,120},{... | collective-permute-start | bytes 196616 | tf_op jit(solution)/shard_map/ppermute | solution.py:36
  66.9 9.4 %collective-permute-start.11 = (bf16[2,128,256]{2,1,0:T(8,128)(2,1)S(1)}, bf16[2,128,256]{2,1,0:T(8,128)(2,1)S(1)}, u32[]{:S(2)}, u32[]{:S(2)}) collective-permute-start(bf16[2,128,256]{2,1,0:T(8,128)(2,1)S(1)} %pad_maximum_fusion.1), channel_id=1, source_target_pairs={{0,16},{8,24},{16,32},{24,40},{32,48},{40,56},{48,64},{56,72},{64,... | collective-permute-start | bytes 393224 | tf_op jit(solution)/shard_map/ppermute | solution.py:61
  71.1 7.0 %collective-permute-start.12 = (bf16[2,128,256]{2,1,0:T(8,128)(2,1)S(1)}, bf16[2,128,256]{2,1,0:T(8,128)(2,1)S(1)}, u32[]{:S(2)}, u32[]{:S(2)}) collective-permute-start(bf16[2,128,256]{2,1,0:T(8,128)(2,1)S(1)} %pad_maximum_fusion.1), channel_id=1, source_target_pairs={{0,8},{8,16},{16,24},{24,32},{32,40},{40,48},{48,56},{56,64},{64,7... | collective-permute-start | bytes 393224 | tf_op jit(solution)/shard_map/ppermute | solution.py:61
  79.6 18.4 %all-to-all-start.3 = ((bf16[32,8,640]{2,0,1:T(8,128)(2,1)}), bf16[32,8,640]{2,0,1:T(8,128)(2,1)S(1)}, u32[]{:S(2)}, u32[]{:S(2)}) async-start(bf16[32,8,640]{2,0,1:T(8,128)(2,1)} %bitcast.234), calls=%async_computation.3 | async-start | bytes 655360 | tf_op jit(solution)/shard_map/all_to_all | solution.py:110
  106.5 9.5 %collective-permute-start.21 = (f32[1,128,256]{2,1,0:T(8,128)S(1)}, f32[1,128,256]{2,1,0:T(8,128)S(1)}, u32[]{:S(2)}, u32[]{:S(2)}) collective-permute-start(f32[1,128,256]{2,1,0:T(8,128)S(1)} %fusion.26), channel_id=1, source_target_pairs={{448,0},{456,8},{464,16},{472,24},{480,32},{488,40},{496,48},{504,... | collective-permute-start | bytes 393224 | tf_op jit(solution)/shard_map/ppermute | solution.py:50
  107.8 9.5 %collective-permute-start.20 = (f32[1,128,256]{2,1,0:T(8,128)S(1)}, f32[1,128,256]{2,1,0:T(8,128)S(1)}, u32[]{:S(2)}, u32[]{:S(2)}) collective-permute-start(f32[1,128,256]{2,1,0:T(8,128)S(1)} %fusion.26), channel_id=1, source_target_pairs={{384,0},{392,8},{400,16},{408,24},{416,32},{424,40},{432,48},{440,... | collective-permute-start | bytes 393224 | tf_op jit(solution)/shard_map/ppermute | solution.py:50
  109.1 10.0 %collective-permute-start.19 = (f32[1,128,256]{2,1,0:T(8,128)S(1)}, f32[1,128,256]{2,1,0:T(8,128)S(1)}, u32[]{:S(2)}, u32[]{:S(2)}) collective-permute-start(f32[1,128,256]{2,1,0:T(8,128)S(1)} %fusion.26), channel_id=1, source_target_pairs={{320,0},{328,8},{336,16},{344,24},{352,32},{360,40},{368,48},{376,... | collective-permute-start | bytes 393224 | tf_op jit(solution)/shard_map/ppermute | solution.py:50
  110.4 18.5 %collective-permute-start.18 = (f32[1,128,256]{2,1,0:T(8,128)S(1)}, f32[1,128,256]{2,1,0:T(8,128)S(1)}, u32[]{:S(2)}, u32[]{:S(2)}) collective-permute-start(f32[1,128,256]{2,1,0:T(8,128)S(1)} %fusion.26), channel_id=1, source_target_pairs={{256,0},{264,8},{272,16},{280,24},{288,32},{296,40},{304,48},{312,... | collective-permute-start | bytes 393224 | tf_op jit(solution)/shard_map/ppermute | solution.py:50
  111.8 18.4 %collective-permute-start.17 = (f32[1,128,256]{2,1,0:T(8,128)S(1)}, f32[1,128,256]{2,1,0:T(8,128)S(1)}, u32[]{:S(2)}, u32[]{:S(2)}) collective-permute-start(f32[1,128,256]{2,1,0:T(8,128)S(1)} %fusion.26), channel_id=1, source_target_pairs={{192,0},{200,8},{208,16},{216,24},{224,32},{232,40},{240,48},{248,... | collective-permute-start | bytes 393224 | tf_op jit(solution)/shard_map/ppermute | solution.py:50
  116.0 14.2 %collective-permute-start.16 = (f32[1,128,256]{2,1,0:T(8,128)S(1)}, f32[1,128,256]{2,1,0:T(8,128)S(1)}, u32[]{:S(2)}, u32[]{:S(2)}) collective-permute-start(f32[1,128,256]{2,1,0:T(8,128)S(1)} %fusion.26), channel_id=1, source_target_pairs={{128,0},{136,8},{144,16},{152,24},{160,32},{168,40},{176,48},{184,... | collective-permute-start | bytes 393224 | tf_op jit(solution)/shard_map/ppermute | solution.py:50
  117.3 12.9 %collective-permute-start.15 = (f32[1,128,256]{2,1,0:T(8,128)S(1)}, f32[1,128,256]{2,1,0:T(8,128)S(1)}, u32[]{:S(2)}, u32[]{:S(2)}) collective-permute-start(f32[1,128,256]{2,1,0:T(8,128)S(1)} %fusion.26), channel_id=1, source_target_pairs={{64,0},{72,8},{80,16},{88,24},{96,32},{104,40},{112,48},{120,56},{... | collective-permute-start | bytes 393224 | tf_op jit(solution)/shard_map/ppermute | solution.py:50
  119.1 30.5 %collective-permute-start.13 = (f32[2,128,256]{2,1,0:T(8,128)S(1)}, f32[2,128,256]{2,1,0:T(8,128)S(1)}, u32[]{:S(2)}, u32[]{:S(2)}) collective-permute-start(f32[2,128,256]{2,1,0:T(8,128)S(1)} %bitcast.270), channel_id=1, source_target_pairs={{8,0},{16,8},{24,16},{32,24},{40,32},{48,40},{56,48},{64,56},{72,6... | collective-permute-start | bytes 786440 | tf_op jit(solution)/shard_map/ppermute | solution.py:61
  128.9 20.7 %collective-permute-start.14 = (f32[2,128,256]{2,1,0:T(8,128)S(1)}, f32[2,128,256]{2,1,0:T(8,128)S(1)}, u32[]{:S(2)}, u32[]{:S(2)}) collective-permute-start(f32[2,128,256]{2,1,0:T(8,128)S(1)} %bitcast.269), channel_id=1, source_target_pairs={{16,0},{24,8},{32,16},{40,24},{48,32},{56,40},{64,48},{72,56},{80,... | collective-permute-start | bytes 786440 | tf_op jit(solution)/shard_map/ppermute | solution.py:61
  130.3 7.6 %collective-permute-start.24 = (f32[1,128,256]{2,1,0:T(8,128)S(1)}, f32[1,128,256]{2,1,0:T(8,128)S(1)}, u32[]{:S(2)}, u32[]{:S(2)}) collective-permute-start(f32[1,128,256]{2,1,0:T(8,128)S(1)} %add_add_fusion.1), channel_id=1, source_target_pairs={{48,0},{56,8},{49,1},{57,9},{50,2},{58,10},{51,3},{59,11},{52,4},{... | collective-permute-start | bytes 393224 | tf_op jit(solution)/shard_map/ppermute | solution.py:50
  131.6 11.6 %collective-permute-start.23 = (f32[1,128,256]{2,1,0:T(8,128)S(1)}, f32[1,128,256]{2,1,0:T(8,128)S(1)}, u32[]{:S(2)}, u32[]{:S(2)}) collective-permute-start(f32[1,128,256]{2,1,0:T(8,128)S(1)} %add_add_fusion.1), channel_id=1, source_target_pairs={{32,0},{40,8},{33,1},{41,9},{34,2},{42,10},{35,3},{43,11},{36,4},{... | collective-permute-start | bytes 393224 | tf_op jit(solution)/shard_map/ppermute | solution.py:50
  132.9 14.3 %collective-permute-start.22 = (f32[1,128,256]{2,1,0:T(8,128)S(1)}, f32[1,128,256]{2,1,0:T(8,128)S(1)}, u32[]{:S(2)}, u32[]{:S(2)}) collective-permute-start(f32[1,128,256]{2,1,0:T(8,128)S(1)} %add_add_fusion.1), channel_id=1, source_target_pairs={{16,0},{24,8},{17,1},{25,9},{18,2},{26,10},{19,3},{27,11},{20,4},{... | collective-permute-start | bytes 393224 | tf_op jit(solution)/shard_map/ppermute | solution.py:50
  147.3 3.3 %collective-permute-start.25 = (f32[1,128,256]{2,1,0:T(8,128)S(1)}, f32[1,128,256]{2,1,0:T(8,128)S(1)}, u32[]{:S(2)}, u32[]{:S(2)}) collective-permute-start(f32[1,128,256]{2,1,0:T(8,128)S(1)} %add_add_fusion), channel_id=1, source_target_pairs={{8,0},{9,1},{10,2},{11,3},{12,4},{13,5},{14,6},{15,7}} | collective-permute-start | bytes 393224 | tf_op jit(solution)/shard_map/ppermute | solution.py:50
  151.2 14.3 %all-to-all-start.6 = ((bf16[8,32,128]{2,1,0:T(8,128)(2,1)}), bf16[8,32,128]{2,1,0:T(8,128)(2,1)S(1)}, u32[]{:S(2)}, u32[]{:S(2)}) async-start(bf16[8,32,128]{2,1,0:T(8,128)(2,1)} %bitcast.69), calls=%async_computation.6 | async-start | bytes 131072 | tf_op jit(solution)/shard_map/all_to_all | solution.py:192
  165.5 12.4 %all-to-all-start.5 = ((bf16[8,32,128]{2,1,0:T(8,128)(2,1)}), bf16[8,32,128]{2,1,0:T(8,128)(2,1)S(1)}, u32[]{:S(2)}, u32[]{:S(2)}) async-start(bf16[8,32,128]{2,1,0:T(8,128)(2,1)} %bitcast.67), calls=%async_computation.5 | async-start | bytes 131072 | tf_op jit(solution)/shard_map/all_to_all | solution.py:191
  177.9 13.6 %all-to-all-start.4 = ((bf16[8,32,640]{2,1,0:T(8,128)(2,1)}), bf16[8,32,640]{2,1,0:T(8,128)(2,1)S(1)}, u32[]{:S(2)}, u32[]{:S(2)}) async-start(bf16[8,32,640]{2,1,0:T(8,128)(2,1)} %bitcast.43), calls=%async_computation.4 | async-start | bytes 655360 | tf_op jit(solution)/shard_map/all_to_all | solution.py:190

commit v2 on v1

--- a/solution.py
+++ b/solution.py
@@ -43,9 +43,22 @@
     return value
 
 
+def binary_levels(size):
+    levels = []
+    for stride, radix in tree_levels(size):
+        if radix & (radix - 1) == 0:
+            while radix > 1:
+                levels.append((stride, 2))
+                stride *= 2
+                radix //= 2
+        else:
+            levels.append((stride, radix))
+    return levels
+
+
 def tree_total(value, axis):
     size = lax.axis_size(axis)
-    for stride, radix in reversed(tree_levels(size)):
+    for stride, radix in reversed(tree_levels(size)[:-1] + binary_levels(size)[-3:]):
         got = [
             lax.ppermute(value, axis, [(j + k * stride, j) for j in range(stride)])
             for k in range(1, radix)
@@ -103,12 +116,25 @@
 
 
 def shards(query_rows, key_rows, value_rows, out_grads, lengths, ancestors):
-    head_query, head_key, head_value, head_grad = (
-        lax.all_to_all(query_rows, "head", split_axis=1, concat_axis=0, tiled=True),
-        lax.all_to_all(key_rows, "head", split_axis=1, concat_axis=0, tiled=True),
-        lax.all_to_all(value_rows, "head", split_axis=1, concat_axis=0, tiled=True),
-        lax.all_to_all(out_grads, "head", split_axis=1, concat_axis=0, tiled=True),
-    )
+    head_groups = lax.axis_size("head")
+    width_q = query_rows.shape[1] // head_groups
+    width_k = key_rows.shape[1] // head_groups
+    rows_in = query_rows.shape[0]
+    packed = jnp.concatenate(
+        [
+            query_rows.reshape(rows_in, head_groups, width_q),
+            key_rows.reshape(rows_in, head_groups, width_k),
+            value_rows.reshape(rows_in, head_groups, width_k),
+            out_grads.reshape(rows_in, head_groups, width_q),
+        ],
+        axis=2,
+    )
+    moved = lax.all_to_all(packed, "head", split_axis=1, concat_axis=0, tiled=True)
+    moved = moved.reshape(moved.shape[0], moved.shape[2])
+    head_query = moved[:, :width_q]
+    head_key = moved[:, width_q : width_q + width_k]
+    head_value = moved[:, width_q + width_k : width_q + 2 * width_k]
+    head_grad = moved[:, width_q + 2 * width_k :]
     row_count = head_query.shape[0]
     tiles_here = row_count // TILE
     kv_width = head_key.shape[1]
@@ -186,11 +212,13 @@
     key_out = (total[:, :, :kv_width] * scaling).astype(jnp.bfloat16).reshape(row_count, kv_width)
     value_out = total[:, :, kv_width:].astype(jnp.bfloat16).reshape(row_count, kv_width)
     query_out = jnp.concatenate(query_parts, axis=0)
-    query_grads, key_grads, value_grads = (
-        lax.all_to_all(query_out, "head", split_axis=0, concat_axis=1, tiled=True),
-        lax.all_to_all(key_out, "head", split_axis=0, concat_axis=1, tiled=True),
-        lax.all_to_all(value_out, "head", split_axis=0, concat_axis=1, tiled=True),
-    )
+    joined = jnp.concatenate([query_out, key_out, value_out], axis=1)
+    joined = joined.reshape(joined.shape[0], 1, joined.shape[1])
+    back = lax.all_to_all(joined, "head", split_axis=0, concat_axis=1, tiled=True)
+    rows_out = back.shape[0]
+    query_grads = back[:, :, :width_q].reshape(rows_out, head_groups * width_q)
+    key_grads = back[:, :, width_q : width_q + width_k].reshape(rows_out, head_groups * width_k)
+    value_grads = back[:, :, width_q + width_k :].reshape(rows_out, head_groups * width_k)
     return (query_grads, key_grads, value_grads)
 
 

time: 195 us -> 158 us (0.81)
  starting transfers between devices: 94.1 us -> 50.8 us
  waiting for transfers between devices: 64.9 us -> 49.4 us
  blocking collectives: 0 us -> 15.4 us
  local copies, waits for them, and re-layouts: 17.1 us -> 22.4 us
    all_to_all x7 -> x1, waiting for transfers between devices: 43.2 us -> 7.94 us  [shards(): lax.all_to_all(packed, 'head', split_axis=1, concat_axis=0, tiled=True)]
    all_to_all x7 -> x1, starting transfers between devices: 44.1 us -> 13.3 us  [shards(): lax.all_to_all(packed, 'head', split_axis=1, concat_axis=0, tiled=True)]
    all_to_all x0 -> x1, blocking collectives: none -> 15.4 us  [shards(): lax.all_to_all(joined, 'head', split_axis=0, concat_axis=1, tiled=True)]
    ppermute x11 -> x7, waiting for transfers between devices: 13.2 us -> 27.6 us  [tree_total(): lax.ppermute(value, axis, [(j + k * stride, j) for j in range(stride)])]
    ppermute x4, starting transfers between devices: 20.4 us -> 12.6 us  [passed_along(): return lax.ppermute(block, axis, route)]
    all_to_all x7 -> x0, local copies, waits for them, and re-layouts: 6.62 us -> none  [the longest x1 1.72 us: shards(): lax.all_to_all(query_rows, 'head', split_axis=1, concat_axis=0, tiled=True)]
    unnamed x8 -> x57, local copies, waits for them, and re-layouts: 1.83 us -> 7.82 us
    ppermute x11, waiting for transfers between devices: 6.72 us -> 12 us  [tree_spread(): lax.ppermute(value, axis, [(j, j + k * stride) for j in range(stride)])]
  transfers between devices with their start and end apart: 33 -> 23, of which waited for: 14 -> 10; matrix products, arithmetic and copies ran while one was open for 11% -> 8% of each run, Pallas kernels for 0% -> 0%
where the time goes in v2:
time: 158 us; the launch traced here: 157 us
  starting transfers between devices  50.8 us (32%)
  waiting for transfers between devices  49.4 us (31%)
  local copies, waits for them, and re-layouts  22.4 us (14%)
  blocking collectives  15.4 us (10%)
  other arithmetic  8.73 us (6%)
  matrix products  8.55 us (5%)
    ppermute x7, waiting for transfers between devices, tree_total(): lax.ppermute(value, axis, [(j + k * stride, j) for j in range(stride)])  27.6 us
    all_to_all x1, blocking collectives, shards(): lax.all_to_all(joined, 'head', split_axis=0, concat_axis=1, tiled=True)  15.4 us
    ppermute x11, starting transfers between devices, tree_spread(): lax.ppermute(value, axis, [(j, j + k * stride) for j in range(stride)])  14.5 us
    all_to_all x1, starting transfers between devices, shards(): lax.all_to_all(packed, 'head', split_axis=1, concat_axis=0, tiled=True)  13.3 us
    ppermute x4, starting transfers between devices, passed_along(): return lax.ppermute(block, axis, route)  12.6 us
    ppermute x11, waiting for transfers between devices, tree_spread(): lax.ppermute(value, axis, [(j, j + k * stride) for j in range(stride)])  12 us
    ppermute x7, starting transfers between devices, tree_total(): lax.ppermute(value, axis, [(j + k * stride, j) for j in range(stride)])  10.4 us
    all_to_all x1, waiting for transfers between devices, shards(): lax.all_to_all(packed, 'head', split_axis=1, concat_axis=0, tiled=True)  7.94 us
  transfers between devices with their start and end apart: 23, of which 10 were waited for; matrix products, arithmetic and copies ran while one was open for 8% of the time, Pallas kernels for 0%

profile of v2, /device:TPU:1, one launch (start us, length us, event | category | flops | bytes accessed | tf_op | source)
XLA Modules:
  0.0 156.7 jit_solution(806871855996727042)
XLA Ops:
  2.4 1.0 copy.144
  3.4 1.0 copy.147
  4.5 1.1 copy.99
  5.6 13.3 %all-to-all-start = ((bf16[32,8,1536]{2,0,1:T(8,128)(2,1)}), bf16[32,8,1536]{2,0,1:T(8,128)(2,1)S(1)}, u32[]{:S(2)}, u32[]{:S(2)}) async-start(bf16[32,8,1536]{2,0,1:T(8,128)(2,1)} %copy.99), calls=%async_computation | async-start | bytes 1572864 | tf_op jit(solution)/shard_map/all_to_all | solution.py:132
  21.4 1.3 iota_compare_fusion.3
  23.1 1.1 broadcast_and_fusion
  25.0 7.9 %all-to-all-done = bf16[32,8,1536]{2,0,1:T(8,128)(2,1)S(1)} async-done(((bf16[32,8,1536]{2,0,1:T(8,128)(2,1)}), bf16[32,8,1536]{2,0,1:T(8,128)(2,1)S(1)}, u32[]{:S(2)}, u32[]{:S(2)}) %all-to-all-start) | async-done | bytes 786464 | tf_op jit(solution)/shard_map/all_to_all | solution.py:132
  33.0 1.3 collective-permute-start
  34.3 10.7 %collective-permute-done = bf16[1,128,256]{2,1,0:T(8,128)(2,1)S(1)} collective-permute-done((bf16[1,128,256]{2,1,0:T(8,128)(2,1)S(1)}, bf16[1,128,256]{2,1,0:T(8,128)(2,1)S(1)}, u32[]{:S(2)}, u32[]{:S(2)}) %collective-permute-start) | collective-permute-done | bytes 65568 | tf_op jit(solution)/shard_map/ppermute | solution.py:36
  45.0 1.3 collective-permute-start.3
  46.3 1.6 %collective-permute-start.2 = (bf16[1,128,256]{2,1,0:T(8,128)(2,1)S(1)}, bf16[1,128,256]{2,1,0:T(8,128)(2,1)S(1)}, u32[]{:S(2)}, u32[]{:S(2)}) collective-permute-start(bf16[1,128,256]{2,1,0:T(8,128)(2,1)S(1)} %broadcast_select_fusion.2), channel_id=1, source_target_pairs={{0,32},{8,40},{1,33},{9,41},{2,34},{10,42},{3,35},{11,43},{4,36},{... | collective-permute-start | bytes 196616 | tf_op jit(solution)/shard_map/ppermute | solution.py:36
  47.9 1.3 collective-permute-start.1
  49.8 1.3 collective-permute-done.1
  51.1 1.3 collective-permute-start.10
  52.4 1.3 collective-permute-start.9
  55.8 1.3 collective-permute-start.8
  57.1 1.3 collective-permute-start.7
  58.4 1.3 collective-permute-start.6
  59.7 1.3 collective-permute-start.5
  61.0 1.3 collective-permute-start.4
  62.3 4.1 %collective-permute-start.11 = (bf16[2,128,256]{2,1,0:T(8,128)(2,1)S(1)}, bf16[2,128,256]{2,1,0:T(8,128)(2,1)S(1)}, u32[]{:S(2)}, u32[]{:S(2)}) collective-permute-start(bf16[2,128,256]{2,1,0:T(8,128)(2,1)S(1)} %pad_maximum_fusion.1), channel_id=1, source_target_pairs={{0,16},{8,24},{16,32},{24,40},{32,48},{40,56},{48,64},{56,72},{64,... | collective-permute-start | bytes 393224 | tf_op jit(solution)/shard_map/ppermute | solution.py:74
  66.5 3.6 %collective-permute-start.12 = (bf16[2,128,256]{2,1,0:T(8,128)(2,1)S(1)}, bf16[2,128,256]{2,1,0:T(8,128)(2,1)S(1)}, u32[]{:S(2)}, u32[]{:S(2)}) collective-permute-start(bf16[2,128,256]{2,1,0:T(8,128)(2,1)S(1)} %pad_maximum_fusion.1), channel_id=1, source_target_pairs={{0,8},{8,16},{16,24},{24,32},{32,40},{40,48},{48,56},{56,64},{64,7... | collective-permute-start | bytes 393224 | tf_op jit(solution)/shard_map/ppermute | solution.py:74
  70.2 1.8 %collective-permute-done.12 = bf16[2,128,256]{2,1,0:T(8,128)(2,1)S(1)} collective-permute-done((bf16[2,128,256]{2,1,0:T(8,128)(2,1)S(1)}, bf16[2,128,256]{2,1,0:T(8,128)(2,1)S(1)}, u32[]{:S(2)}, u32[]{:S(2)}) %collective-permute-start.12) | collective-permute-done | bytes 131104 | tf_op jit(solution)/shard_map/ppermute | solution.py:74
  77.5 1.0 copy.117
  78.4 1.9 %fusion.3 = (f32[5,128]{1,0:T(8,128)S(1)}, f32[896,128,5]{1,0,2:T(8,128)S(1)}) fusion(f32[5,128]{1,0:T(8,128)S(1)} %log_add_fusion.1, f32[896,128,5]{1,0,2:T(8,128)S(1)} %get-tuple-element.51, pred[128,896]{0,1:T(8,128)(4,1)S(1)} %get-tuple-element.43, pred[128,896]{0,1:T(8,128)(4,1)S(1)} %get-tuple-element.42, bf16[896,128,1]{1,0,2:T(8,128)(2,1)} %bitcast.276, ...), kind=kOutput, calls=%fused_computation.14 | convolution fusion | flops 150240640 | bytes 5215232 | tf_op jit(solution)/shard_map/igrd,jgd->grij/dot_general | solution.py:99
  80.3 0.9 fusion.10
  81.2 1.0 copy-done.2
  82.7 1.0 copy.115
  85.4 1.0 copy.121
  86.4 0.9 fusion
  87.4 0.9 fusion.11
  90.2 1.5 collective-permute-start.15
  93.8 7.5 %collective-permute-done.15 = f32[1,128,256]{2,1,0:T(8,128)S(1)} collective-permute-done((f32[1,128,256]{2,1,0:T(8,128)S(1)}, f32[1,128,256]{2,1,0:T(8,128)S(1)}, u32[]{:S(2)}, u32[]{:S(2)}) %collective-permute-start.15) | collective-permute-done | bytes 131104 | tf_op jit(solution)/shard_map/ppermute | solution.py:63
  101.3 1.4 collective-permute-start.16
  103.0 6.9 %collective-permute-done.16 = f32[1,128,256]{2,1,0:T(8,128)S(1)} collective-permute-done((f32[1,128,256]{2,1,0:T(8,128)S(1)}, f32[1,128,256]{2,1,0:T(8,128)S(1)}, u32[]{:S(2)}, u32[]{:S(2)}) %collective-permute-start.16) | collective-permute-done | bytes 131104 | tf_op jit(solution)/shard_map/ppermute | solution.py:63
  110.0 1.3 collective-permute-start.17
  111.7 3.6 %collective-permute-start.13 = (f32[2,128,256]{2,1,0:T(8,128)S(1)}, f32[2,128,256]{2,1,0:T(8,128)S(1)}, u32[]{:S(2)}, u32[]{:S(2)}) collective-permute-start(f32[2,128,256]{2,1,0:T(8,128)S(1)} %bitcast.274), channel_id=1, source_target_pairs={{8,0},{16,8},{24,16},{32,24},{40,32},{48,40},{56,48},{64,56},{72,6... | collective-permute-start | bytes 786440 | tf_op jit(solution)/shard_map/ppermute | solution.py:74
  115.3 1.3 collective-permute-start.14
  116.6 1.3 collective-permute-start.20
  117.9 1.3 collective-permute-start.19
  119.2 1.3 collective-permute-start.18
  121.3 5.7 %collective-permute-done.20 = f32[1,128,256]{2,1,0:T(8,128)S(1)} collective-permute-done((f32[1,128,256]{2,1,0:T(8,128)S(1)}, f32[1,128,256]{2,1,0:T(8,128)S(1)}, u32[]{:S(2)}, u32[]{:S(2)}) %collective-permute-start.20) | collective-permute-done | bytes 131104 | tf_op jit(solution)/shard_map/ppermute | solution.py:63
  127.0 3.2 %collective-permute-done.19 = f32[1,128,256]{2,1,0:T(8,128)S(1)} collective-permute-done((f32[1,128,256]{2,1,0:T(8,128)S(1)}, f32[1,128,256]{2,1,0:T(8,128)S(1)}, u32[]{:S(2)}, u32[]{:S(2)}) %collective-permute-start.19) | collective-permute-done | bytes 131104 | tf_op jit(solution)/shard_map/ppermute | solution.py:63
  130.2 3.4 %collective-permute-done.18 = f32[1,128,256]{2,1,0:T(8,128)S(1)} collective-permute-done((f32[1,128,256]{2,1,0:T(8,128)S(1)}, f32[1,128,256]{2,1,0:T(8,128)S(1)}, u32[]{:S(2)}, u32[]{:S(2)}) %collective-permute-start.18) | collective-permute-done | bytes 131104 | tf_op jit(solution)/shard_map/ppermute | solution.py:63
  133.7 2.3 %collective-permute-start.21 = (f32[1,128,256]{2,1,0:T(8,128)S(1)}, f32[1,128,256]{2,1,0:T(8,128)S(1)}, u32[]{:S(2)}, u32[]{:S(2)}) collective-permute-start(f32[1,128,256]{2,1,0:T(8,128)S(1)} %add_add_fusion), channel_id=1, source_target_pairs={{8,0},{9,1},{10,2},{11,3},{12,4},{13,5},{14,6},{15,7}} | collective-permute-start | bytes 393224 | tf_op jit(solution)/shard_map/ppermute | solution.py:63
  136.1 0.9 collective-permute-done.21
  137.6 0.9 reduce.16
  138.7 15.4 %all_to_all.33 = bf16[8,2,14336]{2,1,0:T(2,128)(2,1)S(1)} all-to-all(bf16[8,2,14336]{2,1,0:T(2,128)(2,1)S(1)} %reshape.444), channel_id=1, replica_groups=mesh['blk'=64,'head'=8] {'head'}, dimensions={0} | all-to-all | bytes 917504 | tf_op jit(solution)/shard_map/all_to_all | solution.py:217
  (149 shorter events, 24.8 us)
Async XLA Ops:
  0.6 18.3 %copy-start = (s32[128,5]{0,1:T(8,128)S(1)}, s32[128,5]{0,1:T(8,128)}, u32[]{:S(2)}) copy-start(s32[128,5]{0,1:T(8,128)} %param.17) | copy-start | bytes 7684
  4.4 15.0 %copy-start.1 = (s32[128]{0:T(128)S(1)}, s32[128]{0:T(128)}, u32[]{:S(2)}) copy-start(s32[128]{0:T(128)} %param.16) | copy-start | bytes 1540
  5.6 27.3 %all-to-all-start = ((bf16[32,8,1536]{2,0,1:T(8,128)(2,1)}), bf16[32,8,1536]{2,0,1:T(8,128)(2,1)S(1)}, u32[]{:S(2)}, u32[]{:S(2)}) async-start(bf16[32,8,1536]{2,0,1:T(8,128)(2,1)} %copy.99), calls=%async_computation | async-start | bytes 1572864 | tf_op jit(solution)/shard_map/all_to_all | solution.py:132
  33.0 12.1 %collective-permute-start = (bf16[1,128,256]{2,1,0:T(8,128)(2,1)S(1)}, bf16[1,128,256]{2,1,0:T(8,128)(2,1)S(1)}, u32[]{:S(2)}, u32[]{:S(2)}) collective-permute-start(bf16[1,128,256]{2,1,0:T(8,128)(2,1)S(1)} %fusion.26), channel_id=1, source_target_pairs={{0,8},{1,9},{2,10},{3,11},{4,12},{5,13},{6,14},{7,15}} | collective-permute-start | bytes 196616 | tf_op jit(solution)/shard_map/ppermute | solution.py:36
  45.0 4.8 %collective-permute-start.3 = (bf16[1,128,256]{2,1,0:T(8,128)(2,1)S(1)}, bf16[1,128,256]{2,1,0:T(8,128)(2,1)S(1)}, u32[]{:S(2)}, u32[]{:S(2)}) collective-permute-start(bf16[1,128,256]{2,1,0:T(8,128)(2,1)S(1)} %broadcast_select_fusion.2), channel_id=1, source_target_pairs={{0,48},{8,56},{1,49},{9,57},{2,50},{10,58},{3,51},{11,59},{4,52},{... | collective-permute-start | bytes 196616 | tf_op jit(solution)/shard_map/ppermute | solution.py:36
  46.3 3.5 %collective-permute-start.2 = (bf16[1,128,256]{2,1,0:T(8,128)(2,1)S(1)}, bf16[1,128,256]{2,1,0:T(8,128)(2,1)S(1)}, u32[]{:S(2)}, u32[]{:S(2)}) collective-permute-start(bf16[1,128,256]{2,1,0:T(8,128)(2,1)S(1)} %broadcast_select_fusion.2), channel_id=1, source_target_pairs={{0,32},{8,40},{1,33},{9,41},{2,34},{10,42},{3,35},{11,43},{4,36},{... | collective-permute-start | bytes 196616 | tf_op jit(solution)/shard_map/ppermute | solution.py:36
  47.9 3.2 %collective-permute-start.1 = (bf16[1,128,256]{2,1,0:T(8,128)(2,1)S(1)}, bf16[1,128,256]{2,1,0:T(8,128)(2,1)S(1)}, u32[]{:S(2)}, u32[]{:S(2)}) collective-permute-start(bf16[1,128,256]{2,1,0:T(8,128)(2,1)S(1)} %broadcast_select_fusion.2), channel_id=1, source_target_pairs={{0,16},{8,24},{1,17},{9,25},{2,18},{10,26},{3,19},{11,27},{4,20},{... | collective-permute-start | bytes 196616 | tf_op jit(solution)/shard_map/ppermute | solution.py:36
  51.1 8.5 %collective-permute-start.10 = (bf16[1,128,256]{2,1,0:T(8,128)(2,1)S(1)}, bf16[1,128,256]{2,1,0:T(8,128)(2,1)S(1)}, u32[]{:S(2)}, u32[]{:S(2)}) collective-permute-start(bf16[1,128,256]{2,1,0:T(8,128)(2,1)S(1)} %add_select_fusion.1), channel_id=1, source_target_pairs={{0,448},{8,456},{16,464},{24,472},{32,480},{40,488},{48,496},{56,5... | collective-permute-start | bytes 196616 | tf_op jit(solution)/shard_map/ppermute | solution.py:36
  52.4 8.5 %collective-permute-start.9 = (bf16[1,128,256]{2,1,0:T(8,128)(2,1)S(1)}, bf16[1,128,256]{2,1,0:T(8,128)(2,1)S(1)}, u32[]{:S(2)}, u32[]{:S(2)}) collective-permute-start(bf16[1,128,256]{2,1,0:T(8,128)(2,1)S(1)} %add_select_fusion.1), channel_id=1, source_target_pairs={{0,384},{8,392},{16,400},{24,408},{32,416},{40,424},{48,432},{56,4... | collective-permute-start | bytes 196616 | tf_op jit(solution)/shard_map/ppermute | solution.py:36
  55.8 6.6 %collective-permute-start.8 = (bf16[1,128,256]{2,1,0:T(8,128)(2,1)S(1)}, bf16[1,128,256]{2,1,0:T(8,128)(2,1)S(1)}, u32[]{:S(2)}, u32[]{:S(2)}) collective-permute-start(bf16[1,128,256]{2,1,0:T(8,128)(2,1)S(1)} %add_select_fusion.1), channel_id=1, source_target_pairs={{0,320},{8,328},{16,336},{24,344},{32,352},{40,360},{48,368},{56,3... | collective-permute-start | bytes 196616 | tf_op jit(solution)/shard_map/ppermute | solution.py:36
  57.1 9.4 %collective-permute-start.7 = (bf16[1,128,256]{2,1,0:T(8,128)(2,1)S(1)}, bf16[1,128,256]{2,1,0:T(8,128)(2,1)S(1)}, u32[]{:S(2)}, u32[]{:S(2)}) collective-permute-start(bf16[1,128,256]{2,1,0:T(8,128)(2,1)S(1)} %add_select_fusion.1), channel_id=1, source_target_pairs={{0,256},{8,264},{16,272},{24,280},{32,288},{40,296},{48,304},{56,3... | collective-permute-start | bytes 196616 | tf_op jit(solution)/shard_map/ppermute | solution.py:36
  58.4 11.7 %collective-permute-start.6 = (bf16[1,128,256]{2,1,0:T(8,128)(2,1)S(1)}, bf16[1,128,256]{2,1,0:T(8,128)(2,1)S(1)}, u32[]{:S(2)}, u32[]{:S(2)}) collective-permute-start(bf16[1,128,256]{2,1,0:T(8,128)(2,1)S(1)} %add_select_fusion.1), channel_id=1, source_target_pairs={{0,192},{8,200},{16,208},{24,216},{32,224},{40,232},{48,240},{56,2... | collective-permute-start | bytes 196616 | tf_op jit(solution)/shard_map/ppermute | solution.py:36
  59.7 10.4 %collective-permute-start.5 = (bf16[1,128,256]{2,1,0:T(8,128)(2,1)S(1)}, bf16[1,128,256]{2,1,0:T(8,128)(2,1)S(1)}, u32[]{:S(2)}, u32[]{:S(2)}) collective-permute-start(bf16[1,128,256]{2,1,0:T(8,128)(2,1)S(1)} %add_select_fusion.1), channel_id=1, source_target_pairs={{0,128},{8,136},{16,144},{24,152},{32,160},{40,168},{48,176},{56,1... | collective-permute-start | bytes 196616 | tf_op jit(solution)/shard_map/ppermute | solution.py:36
  61.0 9.1 %collective-permute-start.4 = (bf16[1,128,256]{2,1,0:T(8,128)(2,1)S(1)}, bf16[1,128,256]{2,1,0:T(8,128)(2,1)S(1)}, u32[]{:S(2)}, u32[]{:S(2)}) collective-permute-start(bf16[1,128,256]{2,1,0:T(8,128)(2,1)S(1)} %add_select_fusion.1), channel_id=1, source_target_pairs={{0,64},{8,72},{16,80},{24,88},{32,96},{40,104},{48,112},{56,120},{... | collective-permute-start | bytes 196616 | tf_op jit(solution)/shard_map/ppermute | solution.py:36
  62.3 7.8 %collective-permute-start.11 = (bf16[2,128,256]{2,1,0:T(8,128)(2,1)S(1)}, bf16[2,128,256]{2,1,0:T(8,128)(2,1)S(1)}, u32[]{:S(2)}, u32[]{:S(2)}) collective-permute-start(bf16[2,128,256]{2,1,0:T(8,128)(2,1)S(1)} %pad_maximum_fusion.1), channel_id=1, source_target_pairs={{0,16},{8,24},{16,32},{24,40},{32,48},{40,56},{48,64},{56,72},{64,... | collective-permute-start | bytes 393224 | tf_op jit(solution)/shard_map/ppermute | solution.py:74
  66.5 5.5 %collective-permute-start.12 = (bf16[2,128,256]{2,1,0:T(8,128)(2,1)S(1)}, bf16[2,128,256]{2,1,0:T(8,128)(2,1)S(1)}, u32[]{:S(2)}, u32[]{:S(2)}) collective-permute-start(bf16[2,128,256]{2,1,0:T(8,128)(2,1)S(1)} %pad_maximum_fusion.1), channel_id=1, source_target_pairs={{0,8},{8,16},{16,24},{24,32},{32,40},{40,48},{48,56},{56,64},{64,7... | collective-permute-start | bytes 393224 | tf_op jit(solution)/shard_map/ppermute | solution.py:74
  74.1 9.5 %copy-start.7 = (bf16[7,128,128]{2,1,0:T(8,128)(2,1)}, bf16[7,128,128]{2,1,0:T(8,128)(2,1)S(1)}, u32[]{:S(2)}) copy-start(bf16[7,128,128]{2,1,0:T(8,128)(2,1)S(1)} %get-tuple-element.38) | copy-start | bytes 688132
  75.0 0.7 copy-start.9
  81.2 1.0 copy-start.2
  82.2 1.4 copy-start.11
  82.2 1.4 copy-start.13
  83.6 1.0 copy-start.15
  83.6 1.0 copy-start.18
  84.7 1.8 %copy-start.17 = (bf16[7,128,128]{2,1,0:T(8,128)(2,1)S(1)}, bf16[7,128,128]{2,1,0:T(8,128)(2,1)}, u32[]{:S(2)}) copy-start(bf16[7,128,128]{2,1,0:T(8,128)(2,1)} %get-tuple-element.39) | copy-start | bytes 688132
  84.7 1.8 %copy-start.19 = (bf16[128,640]{0,1:T(8,128)(2,1)S(1)}, bf16[128,640]{0,1:T(8,128)(2,1)}, u32[]{:S(2)}) copy-start(bf16[128,640]{0,1:T(8,128)(2,1)} %copy.108) | copy-start | bytes 491524
  86.4 0.9 copy-start.12
  86.4 1.0 copy-start.16
  87.4 0.9 copy-start.14
  88.3 1.0 copy-start.4
  88.3 1.2 copy-start.5
  88.3 1.3 copy-start.6
  89.6 2.5 %copy-start.20 = (pred[6]{0:T(512)(128)(4,1)S(1)}, pred[6]{0:T(512)(128)(4,1)}, u32[]{:S(2)}) copy-start(pred[6]{0:T(512)(128)(4,1)} %pad_add_fusion.3) | copy-start | bytes 22
  89.6 2.5 %copy-start.21 = (s32[6]{0:T(128)S(1)}, s32[6]{0:T(128)}, u32[]{:S(2)}) copy-start(s32[6]{0:T(128)} %pad_add_fusion.8) | copy-start | bytes 76
  90.2 11.1 %collective-permute-start.15 = (f32[1,128,256]{2,1,0:T(8,128)S(1)}, f32[1,128,256]{2,1,0:T(8,128)S(1)}, u32[]{:S(2)}, u32[]{:S(2)}) collective-permute-start(f32[1,128,256]{2,1,0:T(8,128)S(1)} %fusion.24), channel_id=1, source_target_pairs={{256,0},{264,8},{272,16},{280,24},{288,32},{296,40},{304,48},{312,... | collective-permute-start | bytes 393224 | tf_op jit(solution)/shard_map/ppermute | solution.py:63
  93.0 18.3 %copy-start.3 = (bf16[5,128,896]{1,2,0:T(8,128)(2,1)S(1)}, bf16[5,128,896]{1,2,0:T(8,128)(2,1)}, u32[]{:S(2)}) copy-start(bf16[5,128,896]{1,2,0:T(8,128)(2,1)} %copy-done.2) | copy-start | bytes 3440644
  93.0 18.3 %copy-start.10 = (bf16[7,128,128]{2,1,0:T(8,128)(2,1)S(1)}, bf16[7,128,128]{2,1,0:T(8,128)(2,1)}, u32[]{:S(2)}) copy-start(bf16[7,128,128]{2,1,0:T(8,128)(2,1)} %copy-done.9) | copy-start | bytes 688132
  101.3 19.2 %copy-start.8 = (bf16[7,128,128]{2,1,0:T(8,128)(2,1)S(1)}, bf16[7,128,128]{2,1,0:T(8,128)(2,1)}, u32[]{:S(2)}) copy-start(bf16[7,128,128]{2,1,0:T(8,128)(2,1)} %copy-done.7) | copy-start | bytes 688132
  101.3 8.6 %collective-permute-start.16 = (f32[1,128,256]{2,1,0:T(8,128)S(1)}, f32[1,128,256]{2,1,0:T(8,128)S(1)}, u32[]{:S(2)}, u32[]{:S(2)}) collective-permute-start(f32[1,128,256]{2,1,0:T(8,128)S(1)} %add.124), channel_id=1, source_target_pairs={{128,0},{136,8},{144,16},{152,24},{160,32},{168,40},{176,48},{184,... | collective-permute-start | bytes 393224 | tf_op jit(solution)/shard_map/ppermute | solution.py:63
  110.0 6.6 %collective-permute-start.17 = (f32[1,128,256]{2,1,0:T(8,128)S(1)}, f32[1,128,256]{2,1,0:T(8,128)S(1)}, u32[]{:S(2)}, u32[]{:S(2)}) collective-permute-start(f32[1,128,256]{2,1,0:T(8,128)S(1)} %add.125), channel_id=1, source_target_pairs={{64,0},{72,8},{80,16},{88,24},{96,32},{104,40},{112,48},{120,56},{... | collective-permute-start | bytes 393224 | tf_op jit(solution)/shard_map/ppermute | solution.py:63
  111.7 24.3 %collective-permute-start.13 = (f32[2,128,256]{2,1,0:T(8,128)S(1)}, f32[2,128,256]{2,1,0:T(8,128)S(1)}, u32[]{:S(2)}, u32[]{:S(2)}) collective-permute-start(f32[2,128,256]{2,1,0:T(8,128)S(1)} %bitcast.274), channel_id=1, source_target_pairs={{8,0},{16,8},{24,16},{32,24},{40,32},{48,40},{56,48},{64,56},{72,6... | collective-permute-start | bytes 786440 | tf_op jit(solution)/shard_map/ppermute | solution.py:74
  115.3 20.7 %collective-permute-start.14 = (f32[2,128,256]{2,1,0:T(8,128)S(1)}, f32[2,128,256]{2,1,0:T(8,128)S(1)}, u32[]{:S(2)}, u32[]{:S(2)}) collective-permute-start(f32[2,128,256]{2,1,0:T(8,128)S(1)} %bitcast.273), channel_id=1, source_target_pairs={{16,0},{24,8},{32,16},{40,24},{48,32},{56,40},{64,48},{72,56},{80,... | collective-permute-start | bytes 786440 | tf_op jit(solution)/shard_map/ppermute | solution.py:74
  116.6 10.4 %collective-permute-start.20 = (f32[1,128,256]{2,1,0:T(8,128)S(1)}, f32[1,128,256]{2,1,0:T(8,128)S(1)}, u32[]{:S(2)}, u32[]{:S(2)}) collective-permute-start(f32[1,128,256]{2,1,0:T(8,128)S(1)} %add.126), channel_id=1, source_target_pairs={{48,0},{56,8},{49,1},{57,9},{50,2},{58,10},{51,3},{59,11},{52,4},{... | collective-permute-start | bytes 393224 | tf_op jit(solution)/shard_map/ppermute | solution.py:63
  117.9 12.3 %collective-permute-start.19 = (f32[1,128,256]{2,1,0:T(8,128)S(1)}, f32[1,128,256]{2,1,0:T(8,128)S(1)}, u32[]{:S(2)}, u32[]{:S(2)}) collective-permute-start(f32[1,128,256]{2,1,0:T(8,128)S(1)} %add.126), channel_id=1, source_target_pairs={{32,0},{40,8},{33,1},{41,9},{34,2},{42,10},{35,3},{43,11},{36,4},{... | collective-permute-start | bytes 393224 | tf_op jit(solution)/shard_map/ppermute | solution.py:63
  119.2 14.4 %collective-permute-start.18 = (f32[1,128,256]{2,1,0:T(8,128)S(1)}, f32[1,128,256]{2,1,0:T(8,128)S(1)}, u32[]{:S(2)}, u32[]{:S(2)}) collective-permute-start(f32[1,128,256]{2,1,0:T(8,128)S(1)} %add.126), channel_id=1, source_target_pairs={{16,0},{24,8},{17,1},{25,9},{18,2},{26,10},{19,3},{27,11},{20,4},{... | collective-permute-start | bytes 393224 | tf_op jit(solution)/shard_map/ppermute | solution.py:63
  133.7 3.3 %collective-permute-start.21 = (f32[1,128,256]{2,1,0:T(8,128)S(1)}, f32[1,128,256]{2,1,0:T(8,128)S(1)}, u32[]{:S(2)}, u32[]{:S(2)}) collective-permute-start(f32[1,128,256]{2,1,0:T(8,128)S(1)} %add_add_fusion), channel_id=1, source_target_pairs={{8,0},{9,1},{10,2},{11,3},{12,4},{13,5},{14,6},{15,7}} | collective-permute-start | bytes 393224 | tf_op jit(solution)/shard_map/ppermute | solution.py:63

commit v3 on v2

--- a/solution.py
+++ b/solution.py
@@ -66,6 +66,16 @@
         for extra in got:
             value = value + extra
     return value
+
+
+def gathered_total(value, axis):
+    size = lax.axis_size(axis)
+    if value.size % size:
+        return tree_total(value, axis)
+    pieces = value.reshape(size, value.size // size)
+    mine = jnp.sum(lax.all_to_all(pieces, axis, 0, 0, tiled=True), axis=0)
+    spread_out = jnp.broadcast_to(mine[None], pieces.shape)
+    return lax.all_to_all(spread_out, axis, 0, 0, tiled=True).reshape(value.shape)
 
 
 def passed_along(block, axis, distance):
@@ -203,7 +213,7 @@
             tile_terms[PROMPT_TILES:].reshape(ANC + 1, TILE * 2 * kv_width),
             precision=lax.Precision.HIGHEST,
         )
-    root_total = tree_total(prompt_sum, "blk")
+    root_total = gathered_total(prompt_sum, "blk")
     near_parts = near_sum.reshape(SPAN_DEV + 1, tiles_here, TILE, 2 * kv_width)
     total = near_parts[SPAN_DEV]
     for offset in range(1, SPAN_DEV + 1):

time: 158 us -> 161 us (1.019)
  the two profiles are of different devices: /device:TPU:1 before, /device:TPU:64 now
where the time goes in v3:
time: 161 us; the launch traced here: 160 us
  starting transfers between devices  50.1 us (31%)
  waiting for transfers between devices  39.5 us (25%)
  local copies, waits for them, and re-layouts  26.3 us (16%)
  blocking collectives  21.7 us (13%)
  matrix products  10.7 us (7%)
  other arithmetic  10.1 us (6%)
    all_to_all x1, blocking collectives, shards(): lax.all_to_all(joined, 'head', split_axis=0, concat_axis=1, tiled=True)  21.7 us
    all_to_all x1, waiting for transfers between devices, shards(): lax.all_to_all(packed, 'head', split_axis=1, concat_axis=0, tiled=True)  18.5 us
    ppermute x11, starting transfers between devices, tree_spread(): lax.ppermute(value, axis, [(j, j + k * stride) for j in range(stride)])  12.3 us
    all_to_all x1, starting transfers between devices, shards(): lax.all_to_all(packed, 'head', split_axis=1, concat_axis=0, tiled=True)  11.8 us
    all_to_all x1, starting transfers between devices, gathered_total(): lax.all_to_all(spread_out, axis, 0, 0, tiled=True).reshape(value.shape)  9.46 us
    ppermute x4, starting transfers between devices, passed_along(): return lax.ppermute(block, axis, route)  8.69 us
    unnamed x61, local copies, waits for them, and re-layouts  8.54 us
    all_to_all x1, waiting for transfers between devices, gathered_total(): lax.all_to_all(spread_out, axis, 0, 0, tiled=True).reshape(value.shape)  8.36 us
  transfers between devices with their start and end apart: 18, of which 6 were waited for; matrix products, arithmetic and copies ran while one was open for 10% of the time, Pallas kernels for 0%

profile of v3, /device:TPU:64, one launch (start us, length us, event | category | flops | bytes accessed | tf_op | source)
XLA Modules:
  0.0 159.8 jit_solution(11817606374932263400)
XLA Ops:
  0.6 0.9 copy.146
  1.5 0.9 copy.147
  2.4 1.0 copy.145
  3.4 1.0 copy.148
  4.5 1.1 copy.99
  5.6 11.8 %all-to-all-start = ((bf16[32,8,1536]{2,0,1:T(8,128)(2,1)}), bf16[32,8,1536]{2,0,1:T(8,128)(2,1)S(1)}, u32[]{:S(2)}, u32[]{:S(2)}) async-start(bf16[32,8,1536]{2,0,1:T(8,128)(2,1)} %copy.99), calls=%async_computation | async-start | bytes 1572864 | tf_op jit(solution)/shard_map/all_to_all | solution.py:142
  19.9 1.3 iota_compare_fusion.3
  21.6 1.2 broadcast_and_fusion
  23.1 18.5 %all-to-all-done = bf16[32,8,1536]{2,0,1:T(8,128)(2,1)S(1)} async-done(((bf16[32,8,1536]{2,0,1:T(8,128)(2,1)}), bf16[32,8,1536]{2,0,1:T(8,128)(2,1)S(1)}, u32[]{:S(2)}, u32[]{:S(2)}) %all-to-all-start) | async-done | bytes 786464 | tf_op jit(solution)/shard_map/all_to_all | solution.py:142
  43.7 1.3 collective-permute-start.1
  45.1 5.7 %collective-permute-done.1 = bf16[1,128,256]{2,1,0:T(8,128)(2,1)S(1)} collective-permute-done((bf16[1,128,256]{2,1,0:T(8,128)(2,1)S(1)}, bf16[1,128,256]{2,1,0:T(8,128)(2,1)S(1)}, u32[]{:S(2)}, u32[]{:S(2)}) %collective-permute-start.1) | collective-permute-done | bytes 65568 | tf_op jit(solution)/shard_map/ppermute | solution.py:36
  50.8 1.3 collective-permute-start.10
  52.1 1.3 collective-permute-start.9
  53.5 0.8 copy.108
  54.3 0.8 copy.106
  55.1 0.8 copy.102
  55.9 0.8 copy.100
  56.7 1.3 collective-permute-start.8
  58.0 1.3 collective-permute-start.7
  59.3 1.3 collective-permute-start.6
  60.6 1.3 collective-permute-start.5
  61.9 1.3 collective-permute-start.4
  63.3 2.7 %collective-permute-start.11 = (bf16[2,128,256]{2,1,0:T(8,128)(2,1)S(1)}, bf16[2,128,256]{2,1,0:T(8,128)(2,1)S(1)}, u32[]{:S(2)}, u32[]{:S(2)}) collective-permute-start(bf16[2,128,256]{2,1,0:T(8,128)(2,1)S(1)} %pad_maximum_fusion.1), channel_id=1, source_target_pairs={{0,16},{8,24},{16,32},{24,40},{32,48},{40,56},{48,64},{56,72},{64,... | collective-permute-start | bytes 393224 | tf_op jit(solution)/shard_map/ppermute | solution.py:84
  65.9 2.1 %collective-permute-start.12 = (bf16[2,128,256]{2,1,0:T(8,128)(2,1)S(1)}, bf16[2,128,256]{2,1,0:T(8,128)(2,1)S(1)}, u32[]{:S(2)}, u32[]{:S(2)}) collective-permute-start(bf16[2,128,256]{2,1,0:T(8,128)(2,1)S(1)} %pad_maximum_fusion.1), channel_id=1, source_target_pairs={{0,8},{8,16},{16,24},{24,32},{32,40},{40,48},{48,56},{56,64},{64,7... | collective-permute-start | bytes 393224 | tf_op jit(solution)/shard_map/ppermute | solution.py:84
  68.1 2.0 %collective-permute-done.11 = bf16[2,128,256]{2,1,0:T(8,128)(2,1)S(1)} collective-permute-done((bf16[2,128,256]{2,1,0:T(8,128)(2,1)S(1)}, bf16[2,128,256]{2,1,0:T(8,128)(2,1)S(1)}, u32[]{:S(2)}, u32[]{:S(2)}) %collective-permute-start.11) | collective-permute-done | bytes 131104 | tf_op jit(solution)/shard_map/ppermute | solution.py:84
  70.1 2.1 %collective-permute-done.12 = bf16[2,128,256]{2,1,0:T(8,128)(2,1)S(1)} collective-permute-done((bf16[2,128,256]{2,1,0:T(8,128)(2,1)S(1)}, bf16[2,128,256]{2,1,0:T(8,128)(2,1)S(1)}, u32[]{:S(2)}, u32[]{:S(2)}) %collective-permute-start.12) | collective-permute-done | bytes 131104 | tf_op jit(solution)/shard_map/ppermute | solution.py:84
  73.6 0.9 fusion.56
  77.2 1.0 copy.117
  78.2 0.9 fusion.3
  79.1 0.9 fusion.10
  80.5 1.0 copy.115
  81.5 1.6 %fusion.7 = (f32[5,128]{1,0:T(8,128)S(1)}, f32[896,128,5]{1,0,2:T(8,128)S(1)}) fusion(pred[128,896]{0,1:T(8,128)(4,1)} %get-tuple-element.20, bf16[896,128,1]{1,0,2:T(8,128)(2,1)} %bitcast.243, bf16[128,5,128]{0,2,1:T(8,128)(2,1)} %bitcast.249), kind=kOutput, calls=%fused_computation.22 | convolution fusion | flops 148520320 | bytes 2804224 | tf_op jit(solution)/shard_map/igrd,jgd->grij/dot_general | solution.py:102
  83.7 1.6 convolution_bitcast_fusion
  85.2 2.0 %copy.121 = f32[896,1,128]{2,0,1:T(8,128)} copy(f32[896,1,128]{0,2,1:T(8,128)} %convolution_bitcast_fusion) | data formatting | bytes 917504 | tf_op jit(solution)/shard_map/grij,igrd->jgd/transpose | solution.py:122
  87.2 2.1 %fusion = (f32[5,128]{1,0:T(8,128)S(1)}, f32[896,128,5]{1,0,2:T(8,128)S(1)}) fusion(f32[5,128]{1,0:T(8,128)S(1)} %log_add_fusion, f32[896,128,5]{1,0,2:T(8,128)S(1)} %get-tuple-element.55, pred[128,896]{0,1:T(8,128)(4,1)} %get-tuple-element.20, pred[128,896]{0,1:T(8,128)(4,1)} %get-tuple-element.19, bf16[896,128,1]{1,0,2:T(8,128)(2,1)} %bitcast.274, ...), kind=kOutput, calls=%fused_computation.9 | convolution fusion | flops 150240640 | bytes 5215232 | tf_op jit(solution)/shard_map/igrd,jgd->grij/dot_general | solution.py:109
  89.3 0.9 fusion.11
  90.2 1.0 copy-done.2
  92.5 0.9 fusion.17
  94.7 7.8 %all-to-all-start.1 = ((f32[64,1,512]{2,1,0:T(1,128)}), f32[64,1,512]{2,1,0:T(1,128)S(1)}, u32[]{:S(2)}, u32[]{:S(2)}) async-start(f32[64,1,512]{2,1,0:T(1,128)} %all_to_all.44), calls=%async_computation.1 | async-start | bytes 262144 | tf_op jit(solution)/shard_map/all_to_all | solution.py:76
  103.8 0.8 convolution_add_fusion
  105.7 2.0 %collective-permute-start.13 = (f32[2,128,256]{2,1,0:T(8,128)}, f32[2,128,256]{2,1,0:T(8,128)}, u32[]{:S(2)}, u32[]{:S(2)}) collective-permute-start(f32[2,128,256]{2,1,0:T(8,128)} %bitcast.228), channel_id=1, source_target_pairs={{8,0},{16,8},{24,16},{32,24},{40,32},{48,40},{56,48},{64,56},{72,6... | collective-permute-start | bytes 786440 | tf_op jit(solution)/shard_map/ppermute | solution.py:84
  107.7 1.9 %collective-permute-start.14 = (f32[2,128,256]{2,1,0:T(8,128)S(1)}, f32[2,128,256]{2,1,0:T(8,128)}, u32[]{:S(2)}, u32[]{:S(2)}) collective-permute-start(f32[2,128,256]{2,1,0:T(8,128)S(1)} %bitcast.273), channel_id=1, source_target_pairs={{16,0},{24,8},{32,16},{40,24},{48,32},{56,40},{64,48},{72,56},{80,... | collective-permute-start | bytes 786440 | tf_op jit(solution)/shard_map/ppermute | solution.py:84
  110.1 2.8 %all-to-all-done.1 = f32[64,1,512]{2,1,0:T(1,128)S(1)} async-done(((f32[64,1,512]{2,1,0:T(1,128)}), f32[64,1,512]{2,1,0:T(1,128)S(1)}, u32[]{:S(2)}, u32[]{:S(2)}) %all-to-all-start.1) | async-done | bytes 131104 | tf_op jit(solution)/shard_map/all_to_all | solution.py:76
  113.7 9.5 %all-to-all-start.2 = ((f32[64,1,512]{2,1,0:T(1,128)}), f32[64,1,512]{2,1,0:T(1,128)S(1)}, u32[]{:S(2)}, u32[]{:S(2)}) async-start(f32[64,1,512]{2,1,0:T(1,128)} %broadcast_in_dim.48), calls=%async_computation.2 | async-start | bytes 262144 | tf_op jit(solution)/shard_map/all_to_all | solution.py:78
  123.9 1.1 fusion.22
  125.0 8.4 %all-to-all-done.2 = f32[64,1,512]{2,1,0:T(1,128)S(1)} async-done(((f32[64,1,512]{2,1,0:T(1,128)}), f32[64,1,512]{2,1,0:T(1,128)S(1)}, u32[]{:S(2)}, u32[]{:S(2)}) %all-to-all-start.2) | async-done | bytes 131104 | tf_op jit(solution)/shard_map/all_to_all | solution.py:78
  134.4 0.9 reduce.19
  135.5 21.7 %all_to_all.49 = bf16[8,2,14336]{2,1,0:T(2,128)(2,1)S(1)} all-to-all(bf16[8,2,14336]{2,1,0:T(2,128)(2,1)S(1)} %reshape.472), channel_id=1, replica_groups=mesh['blk'=64,'head'=8] {'head'}, dimensions={0} | all-to-all | bytes 917504 | tf_op jit(solution)/shard_map/all_to_all | solution.py:227
  (144 shorter events, 21.0 us)
Async XLA Ops:
  0.6 16.8 %copy-start = (s32[128,5]{0,1:T(8,128)S(1)}, s32[128,5]{0,1:T(8,128)}, u32[]{:S(2)}) copy-start(s32[128,5]{0,1:T(8,128)} %param.17) | copy-start | bytes 7684
  4.4 13.5 %copy-start.1 = (s32[128]{0:T(128)S(1)}, s32[128]{0:T(128)}, u32[]{:S(2)}) copy-start(s32[128]{0:T(128)} %param.16) | copy-start | bytes 1540
  5.6 36.0 %all-to-all-start = ((bf16[32,8,1536]{2,0,1:T(8,128)(2,1)}), bf16[32,8,1536]{2,0,1:T(8,128)(2,1)S(1)}, u32[]{:S(2)}, u32[]{:S(2)}) async-start(bf16[32,8,1536]{2,0,1:T(8,128)(2,1)} %copy.99), calls=%async_computation | async-start | bytes 1572864 | tf_op jit(solution)/shard_map/all_to_all | solution.py:142
  41.6 0.8 collective-permute-start
  42.4 2.7 %collective-permute-start.3 = (bf16[1,128,256]{2,1,0:T(8,128)(2,1)S(1)}, bf16[1,128,256]{2,1,0:T(8,128)(2,1)S(1)}, u32[]{:S(2)}, u32[]{:S(2)}) collective-permute-start(bf16[1,128,256]{2,1,0:T(8,128)(2,1)S(1)} %broadcast_select_fusion.3), channel_id=1, source_target_pairs={{0,48},{8,56},{1,49},{9,57},{2,50},{10,58},{3,51},{11,59},{4,52},{... | collective-permute-start | bytes 196616 | tf_op jit(solution)/shard_map/ppermute | solution.py:36
  43.1 2.1 %collective-permute-start.2 = (bf16[1,128,256]{2,1,0:T(8,128)(2,1)S(1)}, bf16[1,128,256]{2,1,0:T(8,128)(2,1)S(1)}, u32[]{:S(2)}, u32[]{:S(2)}) collective-permute-start(bf16[1,128,256]{2,1,0:T(8,128)(2,1)S(1)} %broadcast_select_fusion.3), channel_id=1, source_target_pairs={{0,32},{8,40},{1,33},{9,41},{2,34},{10,42},{3,35},{11,43},{4,36},{... | collective-permute-start | bytes 196616 | tf_op jit(solution)/shard_map/ppermute | solution.py:36
  43.7 7.1 %collective-permute-start.1 = (bf16[1,128,256]{2,1,0:T(8,128)(2,1)S(1)}, bf16[1,128,256]{2,1,0:T(8,128)(2,1)S(1)}, u32[]{:S(2)}, u32[]{:S(2)}) collective-permute-start(bf16[1,128,256]{2,1,0:T(8,128)(2,1)S(1)} %broadcast_select_fusion.3), channel_id=1, source_target_pairs={{0,16},{8,24},{1,17},{9,25},{2,18},{10,26},{3,19},{11,27},{4,20},{... | collective-permute-start | bytes 196616 | tf_op jit(solution)/shard_map/ppermute | solution.py:36
  50.8 9.8 %collective-permute-start.10 = (bf16[1,128,256]{2,1,0:T(8,128)(2,1)S(1)}, bf16[1,128,256]{2,1,0:T(8,128)(2,1)S(1)}, u32[]{:S(2)}, u32[]{:S(2)}) collective-permute-start(bf16[1,128,256]{2,1,0:T(8,128)(2,1)S(1)} %add_select_fusion.1), channel_id=1, source_target_pairs={{0,448},{8,456},{16,464},{24,472},{32,480},{40,488},{48,496},{56,5... | collective-permute-start | bytes 196616 | tf_op jit(solution)/shard_map/ppermute | solution.py:36
  52.1 9.8 %collective-permute-start.9 = (bf16[1,128,256]{2,1,0:T(8,128)(2,1)S(1)}, bf16[1,128,256]{2,1,0:T(8,128)(2,1)S(1)}, u32[]{:S(2)}, u32[]{:S(2)}) collective-permute-start(bf16[1,128,256]{2,1,0:T(8,128)(2,1)S(1)} %add_select_fusion.1), channel_id=1, source_target_pairs={{0,384},{8,392},{16,400},{24,408},{32,416},{40,424},{48,432},{56,4... | collective-permute-start | bytes 196616 | tf_op jit(solution)/shard_map/ppermute | solution.py:36
  56.7 6.5 %collective-permute-start.8 = (bf16[1,128,256]{2,1,0:T(8,128)(2,1)S(1)}, bf16[1,128,256]{2,1,0:T(8,128)(2,1)S(1)}, u32[]{:S(2)}, u32[]{:S(2)}) collective-permute-start(bf16[1,128,256]{2,1,0:T(8,128)(2,1)S(1)} %add_select_fusion.1), channel_id=1, source_target_pairs={{0,320},{8,328},{16,336},{24,344},{32,352},{40,360},{48,368},{56,3... | collective-permute-start | bytes 196616 | tf_op jit(solution)/shard_map/ppermute | solution.py:36
  58.0 7.9 %collective-permute-start.7 = (bf16[1,128,256]{2,1,0:T(8,128)(2,1)S(1)}, bf16[1,128,256]{2,1,0:T(8,128)(2,1)S(1)}, u32[]{:S(2)}, u32[]{:S(2)}) collective-permute-start(bf16[1,128,256]{2,1,0:T(8,128)(2,1)S(1)} %add_select_fusion.1), channel_id=1, source_target_pairs={{0,256},{8,264},{16,272},{24,280},{32,288},{40,296},{48,304},{56,3... | collective-permute-start | bytes 196616 | tf_op jit(solution)/shard_map/ppermute | solution.py:36
  59.3 8.7 %collective-permute-start.6 = (bf16[1,128,256]{2,1,0:T(8,128)(2,1)S(1)}, bf16[1,128,256]{2,1,0:T(8,128)(2,1)S(1)}, u32[]{:S(2)}, u32[]{:S(2)}) collective-permute-start(bf16[1,128,256]{2,1,0:T(8,128)(2,1)S(1)} %add_select_fusion.1), channel_id=1, source_target_pairs={{0,192},{8,200},{16,208},{24,216},{32,224},{40,232},{48,240},{56,2... | collective-permute-start | bytes 196616 | tf_op jit(solution)/shard_map/ppermute | solution.py:36
  60.6 7.4 %collective-permute-start.5 = (bf16[1,128,256]{2,1,0:T(8,128)(2,1)S(1)}, bf16[1,128,256]{2,1,0:T(8,128)(2,1)S(1)}, u32[]{:S(2)}, u32[]{:S(2)}) collective-permute-start(bf16[1,128,256]{2,1,0:T(8,128)(2,1)S(1)} %add_select_fusion.1), channel_id=1, source_target_pairs={{0,128},{8,136},{16,144},{24,152},{32,160},{40,168},{48,176},{56,1... | collective-permute-start | bytes 196616 | tf_op jit(solution)/shard_map/ppermute | solution.py:36
  61.9 6.1 %collective-permute-start.4 = (bf16[1,128,256]{2,1,0:T(8,128)(2,1)S(1)}, bf16[1,128,256]{2,1,0:T(8,128)(2,1)S(1)}, u32[]{:S(2)}, u32[]{:S(2)}) collective-permute-start(bf16[1,128,256]{2,1,0:T(8,128)(2,1)S(1)} %add_select_fusion.1), channel_id=1, source_target_pairs={{0,64},{8,72},{16,80},{24,88},{32,96},{40,104},{48,112},{56,120},{... | collective-permute-start | bytes 196616 | tf_op jit(solution)/shard_map/ppermute | solution.py:36
  63.3 6.9 %collective-permute-start.11 = (bf16[2,128,256]{2,1,0:T(8,128)(2,1)S(1)}, bf16[2,128,256]{2,1,0:T(8,128)(2,1)S(1)}, u32[]{:S(2)}, u32[]{:S(2)}) collective-permute-start(bf16[2,128,256]{2,1,0:T(8,128)(2,1)S(1)} %pad_maximum_fusion.1), channel_id=1, source_target_pairs={{0,16},{8,24},{16,32},{24,40},{32,48},{40,56},{48,64},{56,72},{64,... | collective-permute-start | bytes 393224 | tf_op jit(solution)/shard_map/ppermute | solution.py:84
  65.9 6.3 %collective-permute-start.12 = (bf16[2,128,256]{2,1,0:T(8,128)(2,1)S(1)}, bf16[2,128,256]{2,1,0:T(8,128)(2,1)S(1)}, u32[]{:S(2)}, u32[]{:S(2)}) collective-permute-start(bf16[2,128,256]{2,1,0:T(8,128)(2,1)S(1)} %pad_maximum_fusion.1), channel_id=1, source_target_pairs={{0,8},{8,16},{16,24},{24,32},{32,40},{40,48},{48,56},{56,64},{64,7... | collective-permute-start | bytes 393224 | tf_op jit(solution)/shard_map/ppermute | solution.py:84
  73.4 1.9 %copy-start.13 = (pred[128,896]{0,1:T(8,128)(4,1)S(1)}, pred[128,896]{0,1:T(8,128)(4,1)}, u32[]{:S(2)}) copy-start(pred[128,896]{0,1:T(8,128)(4,1)} %get-tuple-element.43) | copy-start | bytes 344068
  73.5 1.9 %copy-start.16 = (bf16[128,640]{0,1:T(8,128)(2,1)S(1)}, bf16[128,640]{0,1:T(8,128)(2,1)}, u32[]{:S(2)}) copy-start(bf16[128,640]{0,1:T(8,128)(2,1)} %copy.100) | copy-start | bytes 491524
  74.7 0.7 copy-start.9
  75.4 1.0 copy-start.20
  75.4 1.0 copy-start.23
  78.2 0.9 copy-start.14
  78.2 1.0 copy-start.21
  79.1 0.9 copy-start.17
  81.5 1.6 %copy-start.11 = (pred[128,896]{0,1:T(8,128)(4,1)S(1)}, pred[128,896]{0,1:T(8,128)(4,1)}, u32[]{:S(2)}) copy-start(pred[128,896]{0,1:T(8,128)(4,1)} %get-tuple-element.20) | copy-start | bytes 344068
  81.5 2.1 %copy-start.18 = (pred[128,896]{0,1:T(8,128)(4,1)S(1)}, pred[128,896]{0,1:T(8,128)(4,1)}, u32[]{:S(2)}) copy-start(pred[128,896]{0,1:T(8,128)(4,1)} %get-tuple-element.19) | copy-start | bytes 344068
  81.5 2.1 %copy-start.22 = (bf16[128,640]{0,1:T(8,128)(2,1)S(1)}, bf16[128,640]{0,1:T(8,128)(2,1)}, u32[]{:S(2)}) copy-start(bf16[128,640]{0,1:T(8,128)(2,1)} %copy.108) | copy-start | bytes 491524
  87.2 2.1 %copy-start.12 = (pred[128,896]{0,1:T(8,128)(4,1)S(1)}, pred[128,896]{0,1:T(8,128)(4,1)}, u32[]{:S(2)}) copy-start(pred[128,896]{0,1:T(8,128)(4,1)} %get-tuple-element.20) | copy-start | bytes 344068
  87.2 2.1 %copy-start.19 = (pred[128,896]{0,1:T(8,128)(4,1)S(1)}, pred[128,896]{0,1:T(8,128)(4,1)}, u32[]{:S(2)}) copy-start(pred[128,896]{0,1:T(8,128)(4,1)} %get-tuple-element.19) | copy-start | bytes 344068
  89.3 1.9 %copy-start.15 = (bf16[128,640]{0,1:T(8,128)(2,1)S(1)}, bf16[128,640]{0,1:T(8,128)(2,1)}, u32[]{:S(2)}) copy-start(bf16[128,640]{0,1:T(8,128)(2,1)} %copy.106) | copy-start | bytes 491524
  90.2 1.0 copy-start.2
  91.2 1.0 copy-start.4
  91.2 1.2 copy-start.5
  91.2 1.3 copy-start.6
  93.5 9.0 %copy-start.7 = (f32[1,6,128,256]{3,2,1,0:T(8,128)S(1)}, f32[1,6,128,256]{3,2,1,0:T(8,128)}, u32[]{:S(2)}) copy-start(f32[1,6,128,256]{3,2,1,0:T(8,128)} %fusion.17) | copy-start | bytes 2359300
  94.7 18.1 %all-to-all-start.1 = ((f32[64,1,512]{2,1,0:T(1,128)}), f32[64,1,512]{2,1,0:T(1,128)S(1)}, u32[]{:S(2)}, u32[]{:S(2)}) async-start(f32[64,1,512]{2,1,0:T(1,128)} %all_to_all.44), calls=%async_computation.1 | async-start | bytes 262144 | tf_op jit(solution)/shard_map/all_to_all | solution.py:76
  103.8 5.8 %copy-start.10 = (bf16[7,128,128]{2,1,0:T(8,128)(2,1)S(1)}, bf16[7,128,128]{2,1,0:T(8,128)(2,1)}, u32[]{:S(2)}) copy-start(bf16[7,128,128]{2,1,0:T(8,128)(2,1)} %copy-done.9) | copy-start | bytes 688132
  104.6 18.5 %copy-start.3 = (bf16[5,128,896]{1,2,0:T(8,128)(2,1)S(1)}, bf16[5,128,896]{1,2,0:T(8,128)(2,1)}, u32[]{:S(2)}) copy-start(bf16[5,128,896]{1,2,0:T(8,128)(2,1)} %copy-done.2) | copy-start | bytes 3440644
  104.7 18.5 %copy-start.8 = (bf16[7,128,128]{2,1,0:T(8,128)(2,1)S(1)}, bf16[7,128,128]{2,1,0:T(8,128)(2,1)}, u32[]{:S(2)}) copy-start(bf16[7,128,128]{2,1,0:T(8,128)(2,1)} %get-tuple-element.38) | copy-start | bytes 688132
  105.7 18.2 %collective-permute-start.13 = (f32[2,128,256]{2,1,0:T(8,128)}, f32[2,128,256]{2,1,0:T(8,128)}, u32[]{:S(2)}, u32[]{:S(2)}) collective-permute-start(f32[2,128,256]{2,1,0:T(8,128)} %bitcast.228), channel_id=1, source_target_pairs={{8,0},{16,8},{24,16},{32,24},{40,32},{48,40},{56,48},{64,56},{72,6... | collective-permute-start | bytes 786440 | tf_op jit(solution)/shard_map/ppermute | solution.py:84
  107.7 16.2 %collective-permute-start.14 = (f32[2,128,256]{2,1,0:T(8,128)S(1)}, f32[2,128,256]{2,1,0:T(8,128)}, u32[]{:S(2)}, u32[]{:S(2)}) collective-permute-start(f32[2,128,256]{2,1,0:T(8,128)S(1)} %bitcast.273), channel_id=1, source_target_pairs={{16,0},{24,8},{32,16},{40,24},{48,32},{56,40},{64,48},{72,56},{80,... | collective-permute-start | bytes 786440 | tf_op jit(solution)/shard_map/ppermute | solution.py:84
  113.7 19.7 %all-to-all-start.2 = ((f32[64,1,512]{2,1,0:T(1,128)}), f32[64,1,512]{2,1,0:T(1,128)S(1)}, u32[]{:S(2)}, u32[]{:S(2)}) async-start(f32[64,1,512]{2,1,0:T(1,128)} %broadcast_in_dim.48), calls=%async_computation.2 | async-start | bytes 262144 | tf_op jit(solution)/shard_map/all_to_all | solution.py:78

commit v4 on v2

--- a/solution.py
+++ b/solution.py
@@ -2,6 +2,8 @@
 import jax.numpy as jnp
 from jax import lax
 from jax.sharding import PartitionSpec as P
+from jax.experimental import pallas as pl
+from jax.experimental.pallas import tpu as pltpu
 
 HD = 128
 TILE = 128
@@ -113,6 +115,76 @@
         "grij,igrd->jgd", weights_low, grads_out, preferred_element_type=jnp.float32
     )
     return (query_part.astype(jnp.bfloat16), key_part, value_part)
+
+
+def tiles_kernel(q_ref, g_ref, k_ref, v_ref, pos_ref, live_ref, dq_ref, dk_ref, dv_ref, *, group, scaling):
+    keys = k_ref[0]
+    values = v_ref[0]
+    rows = lax.broadcasted_iota(jnp.int32, (q_ref.shape[0], keys.shape[0]), 0)
+    seen = pos_ref[0] <= rows
+    kept = seen & (live_ref[0] > 0)
+    dk_acc = jnp.zeros(dk_ref.shape[1:], jnp.float32)
+    dv_acc = jnp.zeros(dv_ref.shape[1:], jnp.float32)
+    width = keys.shape[1]
+    for r in range(group):
+        cols = slice(r * width, (r + 1) * width)
+        qr = q_ref[:, cols]
+        gr = g_ref[:, cols]
+        scores = lax.dot_general(qr, keys, (((1,), (1,)), ((), ())), preferred_element_type=jnp.float32)
+        scores = jnp.where(seen, scores * scaling, -jnp.inf)
+        row_max = jnp.max(scores, axis=1, keepdims=True)
+        log_total = row_max + jnp.log(jnp.sum(jnp.exp(scores - row_max), axis=1, keepdims=True))
+        weights = jnp.where(kept, jnp.exp(scores - log_total), 0.0)
+        weight_grads = lax.dot_general(gr, values, (((1,), (1,)), ((), ())), preferred_element_type=jnp.float32)
+        row_dot = jnp.sum(weights * weight_grads, axis=1, keepdims=True)
+        score_grads = (weights * (weight_grads - row_dot)).astype(jnp.bfloat16)
+        weights_low = weights.astype(jnp.bfloat16)
+        dq = jnp.dot(score_grads, keys, preferred_element_type=jnp.float32) * scaling
+        dq_ref[:, cols] = dq.astype(dq_ref.dtype)
+        dk_acc = dk_acc + lax.dot_general(score_grads, qr, (((0,), (0,)), ((), ())), preferred_element_type=jnp.float32)
+        dv_acc = dv_acc + lax.dot_general(weights_low, gr, (((0,), (0,)), ((), ())), preferred_element_type=jnp.float32)
+    dk_ref[0] = dk_acc
+    dv_ref[0] = dv_acc
+
+
+def tiles_backward(queries, grads_out, keys, values, positions, live, scaling, interpret=False):
+    tiles, key_slots, width = keys.shape
+    group = queries.shape[1] // width
+    rows = queries.shape[0] // tiles
+    row_spec = pl.BlockSpec((rows, queries.shape[1]), lambda t: (t, 0))
+    key_spec = pl.BlockSpec((1, key_slots, width), lambda t: (t, 0, 0))
+    kernel = lambda *refs: tiles_kernel(*refs, group=group, scaling=scaling)
+    return pl.pallas_call(
+        kernel,
+        grid=(tiles,),
+        in_specs=[
+            row_spec,
+            row_spec,
+            key_spec,
+            key_spec,
+            pl.BlockSpec((1, 1, key_slots), lambda t: (t, 0, 0)),
+            pl.BlockSpec((1, rows, 1), lambda t: (t, 0, 0)),
+        ],
+        out_specs=[row_spec, key_spec, key_spec],
+        out_shape=[
+            jax.ShapeDtypeStruct(queries.shape, jnp.bfloat16),
+            jax.ShapeDtypeStruct(keys.shape, jnp.float32),
+            jax.ShapeDtypeStruct(keys.shape, jnp.float32),
+        ],
+        interpret=interpret,
+    )(queries, grads_out, keys, values, positions, live)
+
+
+def column_limits(tile_id, tile_ids, listed, lengths):
+    position = jnp.arange(TILE, dtype=jnp.int32)
+    slot_ok = jnp.concatenate(
+        [jnp.arange(PROMPT_TILES, dtype=jnp.int32) < tile_id, listed >= 0, jnp.ones((1,), bool)]
+    )
+    key_len = jnp.take(lengths, jnp.maximum(tile_ids, 0))
+    key_ok = slot_ok[:, None] & (position[None, :] < key_len[:, None])
+    own_slot = (jnp.arange(KEYT) == KEYT - 1)[:, None]
+    limit = jnp.where(key_ok, jnp.where(own_slot, position[None, :], 0), TILE)
+    return limit.reshape(1, KEYT * TILE)
 
 
 def shards(query_rows, key_rows, value_rows, out_grads, lengths, ancestors):
@@ -162,7 +234,7 @@
     slot_index = jnp.arange(window_slots, dtype=jnp.int32)
     prompt_sum = jnp.zeros((PROMPT_TILES, TILE, 2 * kv_width), jnp.float32)
     near_sum = jnp.zeros((window_slots, TILE * 2 * kv_width), jnp.float32)
-    query_parts = []
+    key_blocks, value_blocks, limits, lives, window_rows = [], [], [], [], []
     for local in range(tiles_here):
         tile_id = first_tile + local
         listed = my_lists[local]
@@ -171,22 +243,27 @@
         own_row = jnp.full((1,), PROMPT_TILES + SPAN_DEV * tiles_here + local, jnp.int32)
         table_rows = jnp.concatenate([prompt_ids, near_rows, own_row])
         chosen = jnp.take(table, table_rows, axis=0)
-        key_block = chosen[:, :, :kv_width].reshape(KEYT * TILE, kv_heads, HD)
-        value_block = chosen[:, :, kv_width:].reshape(KEYT * TILE, kv_heads, HD)
-        allowed = visible_mask(tile_id, tile_ids, listed, lengths)
-        live_rows = jnp.arange(TILE, dtype=jnp.int32) < lengths[tile_id]
-        tile_query = head_query[local * TILE : (local + 1) * TILE].reshape(
-            TILE, kv_heads, group_size, HD
-        )
-        tile_grad = head_grad[local * TILE : (local + 1) * TILE].reshape(
-            TILE, kv_heads, group_size, HD
-        )
-        query_part, key_part, value_part = tile_backward(
-            tile_query, tile_grad, key_block, value_block, allowed, live_rows, scaling
-        )
-        query_parts.append(query_part.reshape(TILE, group_size * kv_width))
+        key_blocks.append(chosen[:, :, :kv_width].reshape(KEYT * TILE, kv_width))
+        value_blocks.append(chosen[:, :, kv_width:].reshape(KEYT * TILE, kv_width))
+        limits.append(column_limits(tile_id, tile_ids, listed, lengths))
+        lives.append((jnp.arange(TILE, dtype=jnp.int32) < lengths[tile_id]).astype(jnp.int32)[:, None])
+        window_rows.append(listed)
+    query_out, key_parts, value_parts = tiles_backward(
+        head_query,
+        head_grad,
+        jnp.stack(key_blocks),
+        jnp.stack(value_blocks),
+        jnp.stack(limits),
+        jnp.stack(lives),
+        scaling,
+    )
+    for local in range(tiles_here):
+        listed = window_rows[local]
         tile_terms = jnp.concatenate(
-            [key_part.reshape(KEYT, TILE, kv_width), value_part.reshape(KEYT, TILE, kv_width)],
+            [
+                key_parts[local].reshape(KEYT, TILE, kv_width),
+                value_parts[local].reshape(KEYT, TILE, kv_width),
+            ],
             axis=2,
         )
         prompt_sum = prompt_sum + tile_terms[:PROMPT_TILES]
@@ -211,7 +288,6 @@
     total = total.at[:PROMPT_TILES].add(jnp.where(block_index == 0, root_total, 0.0))
     key_out = (total[:, :, :kv_width] * scaling).astype(jnp.bfloat16).reshape(row_count, kv_width)
     value_out = total[:, :, kv_width:].astype(jnp.bfloat16).reshape(row_count, kv_width)
-    query_out = jnp.concatenate(query_parts, axis=0)
     joined = jnp.concatenate([query_out, key_out, value_out], axis=1)
     joined = joined.reshape(joined.shape[0], 1, joined.shape[1])
     back = lax.all_to_all(joined, "head", split_axis=0, concat_axis=1, tiled=True)

time: 158 us -> 152 us (0.962)
  the two profiles are of different devices: /device:TPU:1 before, /device:TPU:128 now
where the time goes in v4:
time: 152 us; the launch traced here: 151 us
  waiting for transfers between devices  56.4 us (37%)
  starting transfers between devices  41.9 us (28%)
  blocking collectives  21 us (14%)
  local copies, waits for them, and re-layouts  12.4 us (8%)
  Pallas kernels  9.84 us (6%)
  other arithmetic  6.95 us (5%)
  matrix products  1.59 us (1%)
    all_to_all x1, blocking collectives, shards(): lax.all_to_all(joined, 'head', split_axis=0, concat_axis=1, tiled=True)  21 us
    ppermute x7, waiting for transfers between devices, tree_total(): lax.ppermute(value, axis, [(j + k * stride, j) for j in range(stride)])  20.3 us
    all_to_all x1, waiting for transfers between devices, shards(): lax.all_to_all(packed, 'head', split_axis=1, concat_axis=0, tiled=True)  17.9 us
    ppermute x11, starting transfers between devices, tree_spread(): lax.ppermute(value, axis, [(j, j + k * stride) for j in range(stride)])  12.3 us
    ppermute x4, waiting for transfers between devices, passed_along(): return lax.ppermute(block, axis, route)  12.3 us
    ppermute x4, starting transfers between devices, passed_along(): return lax.ppermute(block, axis, route)  11.2 us
    all_to_all x1, starting transfers between devices, shards(): lax.all_to_all(packed, 'head', split_axis=1, concat_axis=0, tiled=True)  11.1 us
    pallas_call x1, Pallas kernels, tiles_backward(): pl.pallas_call(kernel, grid=(tiles,), in_specs=[row_spec, row_spec, key_s...  9.84 us
  transfers between devices with their start and end apart: 23, of which 9 were waited for; matrix products, arithmetic and copies ran while one was open for 6% of the time, Pallas kernels for 0%

profile of v4, /device:TPU:128, one launch (start us, length us, event | category | flops | bytes accessed | tf_op | source)
XLA Modules:
  0.0 151.4 jit_solution(16638795350690833899)
XLA Ops:
  0.7 1.2 copy_bitcast_fusion
  1.9 1.0 pad_maximum_fusion
  2.9 11.1 %all-to-all-start = ((bf16[32,8,1536]{2,0,1:T(8,128)(2,1)}), bf16[32,8,1536]{2,0,1:T(8,128)(2,1)S(1)}, u32[]{:S(2)}, u32[]{:S(2)}) async-start(bf16[32,8,1536]{2,0,1:T(8,128)(2,1)} %pad_maximum_fusion), calls=%async_computation | async-start | bytes 1572864 | tf_op jit(solution)/shard_map/all_to_all | solution.py:204
  14.3 0.6 gather_fusion.3
  15.0 0.6 gather_fusion.2
  16.5 1.3 iota_compare_fusion.4
  17.8 0.8 copy.51.refs_5_
  19.5 17.9 %all-to-all-done = bf16[32,8,1536]{2,0,1:T(8,128)(2,1)S(1)} async-done(((bf16[32,8,1536]{2,0,1:T(8,128)(2,1)}), bf16[32,8,1536]{2,0,1:T(8,128)(2,1)S(1)}, u32[]{:S(2)}, u32[]{:S(2)}) %all-to-all-start) | async-done | bytes 786464 | tf_op jit(solution)/shard_map/all_to_all | solution.py:204
  37.4 0.7 collective-permute-start
  38.2 0.7 collective-permute-start.1
  38.8 1.3 collective-permute-start.2
  40.1 0.7 collective-permute-start.3
  40.9 5.8 %collective-permute-done.2 = bf16[1,128,256]{2,1,0:T(8,128)(2,1)S(1)} collective-permute-done((bf16[1,128,256]{2,1,0:T(8,128)(2,1)S(1)}, bf16[1,128,256]{2,1,0:T(8,128)(2,1)S(1)}, u32[]{:S(2)}, u32[]{:S(2)}) %collective-permute-start.2) | collective-permute-done | bytes 65568 | tf_op jit(solution)/shard_map/ppermute | solution.py:38
  46.7 1.3 collective-permute-start.10
  48.0 1.3 collective-permute-start.4
  49.3 0.9 fusion.32
  50.2 1.3 collective-permute-start.5
  51.5 1.3 collective-permute-start.6
  52.8 1.3 collective-permute-start.7
  54.1 1.3 collective-permute-start.8
  55.5 1.3 collective-permute-start.9
  56.8 4.3 %collective-permute-start.11 = (bf16[2,128,256]{2,1,0:T(8,128)(2,1)S(1)}, bf16[2,128,256]{2,1,0:T(8,128)(2,1)S(1)}, u32[]{:S(2)}, u32[]{:S(2)}) collective-permute-start(bf16[2,128,256]{2,1,0:T(8,128)(2,1)S(1)} %pad_maximum_fusion.3), channel_id=1, source_target_pairs={{0,16},{8,24},{16,32},{24,40},{32,48},{40,56},{48,64},{56,72},{64,... | collective-permute-start | bytes 393224 | tf_op jit(solution)/shard_map/ppermute | solution.py:76
  61.1 1.9 %collective-permute-start.12 = (bf16[2,128,256]{2,1,0:T(8,128)(2,1)S(1)}, bf16[2,128,256]{2,1,0:T(8,128)(2,1)S(1)}, u32[]{:S(2)}, u32[]{:S(2)}) collective-permute-start(bf16[2,128,256]{2,1,0:T(8,128)(2,1)S(1)} %pad_maximum_fusion.3), channel_id=1, source_target_pairs={{0,8},{8,16},{16,24},{24,32},{32,40},{40,48},{48,56},{56,64},{64,7... | collective-permute-start | bytes 393224 | tf_op jit(solution)/shard_map/ppermute | solution.py:76
  63.7 3.8 %collective-permute-done.12 = bf16[2,128,256]{2,1,0:T(8,128)(2,1)S(1)} collective-permute-done((bf16[2,128,256]{2,1,0:T(8,128)(2,1)S(1)}, bf16[2,128,256]{2,1,0:T(8,128)(2,1)S(1)}, u32[]{:S(2)}, u32[]{:S(2)}) %collective-permute-start.12) | collective-permute-done | bytes 131104 | tf_op jit(solution)/shard_map/ppermute | solution.py:76
  69.1 0.8 pad_maximum_fusion.2.refs_3_
  69.9 0.8 pad_maximum_fusion.1.refs_2_
  70.7 9.8 %shard_map.85 = (bf16[256,640]{1,0:T(8,128)(2,1)}, f32[2,896,128]{2,1,0:T(8,128)}, f32[2,896,128]{2,1,0:T(8,128)}) custom-call(bf16[256,640]{1,0:T(8,128)(2,1)} %get-tuple-element.39.refs_0_, bf16[256,640]{1,0:T(8,128)(2,1)} %get-tuple-element.38.refs_1_, bf16[2,896,128]{2,1,0:T(8,128)(2,1)} %pad_maximum_fusion.1.refs_2_, ...), custom_call_target="tpu_custom_call" | custom-call | tf_op jit(solution)/shard_map/pallas_call | solution.py:157
  80.6 1.3 fusion.30
  82.2 1.3 collective-permute-start.15
  83.9 0.8 fusion.14
  84.7 8.2 %collective-permute-done.15 = f32[1,128,256]{2,1,0:T(8,128)S(1)} collective-permute-done((f32[1,128,256]{2,1,0:T(8,128)S(1)}, f32[1,128,256]{2,1,0:T(8,128)S(1)}, u32[]{:S(2)}, u32[]{:S(2)}) %collective-permute-start.15) | collective-permute-done | bytes 131104 | tf_op jit(solution)/shard_map/ppermute | solution.py:65
  93.0 1.3 collective-permute-start.16
  94.8 7.4 %collective-permute-done.16 = f32[1,128,256]{2,1,0:T(8,128)S(1)} collective-permute-done((f32[1,128,256]{2,1,0:T(8,128)S(1)}, f32[1,128,256]{2,1,0:T(8,128)S(1)}, u32[]{:S(2)}, u32[]{:S(2)}) %collective-permute-start.16) | collective-permute-done | bytes 131104 | tf_op jit(solution)/shard_map/ppermute | solution.py:65
  102.2 1.3 collective-permute-start.17
  103.5 0.8 convolution_add_fusion
  104.3 4.7 %collective-permute-done.17 = f32[1,128,256]{2,1,0:T(8,128)S(1)} collective-permute-done((f32[1,128,256]{2,1,0:T(8,128)S(1)}, f32[1,128,256]{2,1,0:T(8,128)S(1)}, u32[]{:S(2)}, u32[]{:S(2)}) %collective-permute-start.17) | collective-permute-done | bytes 131104 | tf_op jit(solution)/shard_map/ppermute | solution.py:65
  109.1 0.7 collective-permute-start.18
  109.7 1.3 collective-permute-start.19
  111.0 0.7 collective-permute-start.20
  112.0 1.9 %collective-permute-start.13 = (f32[2,128,256]{2,1,0:T(8,128)S(1)}, f32[2,128,256]{2,1,0:T(8,128)S(1)}, u32[]{:S(2)}, u32[]{:S(2)}) collective-permute-start(f32[2,128,256]{2,1,0:T(8,128)S(1)} %bitcast.110), channel_id=1, source_target_pairs={{8,0},{16,8},{24,16},{32,24},{40,32},{48,40},{56,48},{64,56},{72,6... | collective-permute-start | bytes 786440 | tf_op jit(solution)/shard_map/ppermute | solution.py:76
  114.0 3.1 %collective-permute-start.14 = (f32[2,128,256]{2,1,0:T(8,128)S(1)}, f32[2,128,256]{2,1,0:T(8,128)S(1)}, u32[]{:S(2)}, u32[]{:S(2)}) collective-permute-start(f32[2,128,256]{2,1,0:T(8,128)S(1)} %bitcast.111), channel_id=1, source_target_pairs={{16,0},{24,8},{32,16},{40,24},{48,32},{56,40},{64,48},{72,56},{80,... | collective-permute-start | bytes 786440 | tf_op jit(solution)/shard_map/ppermute | solution.py:76
  117.1 0.8 collective-permute-start.21
  117.9 1.5 collective-permute-done.13
  119.4 6.6 %collective-permute-done.14 = f32[2,128,256]{2,1,0:T(8,128)S(1)} collective-permute-done((f32[2,128,256]{2,1,0:T(8,128)S(1)}, f32[2,128,256]{2,1,0:T(8,128)S(1)}, u32[]{:S(2)}, u32[]{:S(2)}) %collective-permute-start.14) | collective-permute-done | bytes 262176 | tf_op jit(solution)/shard_map/ppermute | solution.py:76
  126.7 0.9 reduce.6
  127.8 21.0 %all_to_all.33 = bf16[8,2,14336]{2,1,0:T(2,128)(2,1)S(1)} all-to-all(bf16[8,2,14336]{2,1,0:T(2,128)(2,1)S(1)} %reshape.309), channel_id=1, replica_groups=mesh['blk'=64,'head'=8] {'head'}, dimensions={0} | all-to-all | bytes 917504 | tf_op jit(solution)/shard_map/all_to_all | solution.py:293
  149.4 0.8 copy.61
  150.7 0.6 copy.81
  (92 shorter events, 8.3 us)
Async XLA Ops:
  0.6 1.2 copy-start
  0.6 1.2 copy-start.4
  2.9 11.1 %copy-start.5 = (s32[128,5]{0,1:T(8,128)S(1)}, s32[128,5]{0,1:T(8,128)}, u32[]{:S(2)}) copy-start(s32[128,5]{0,1:T(8,128)} %param.17) | copy-start | bytes 7684
  2.9 11.5 %copy-start.1 = (s32[128]{0:T(128)S(1)}, s32[128]{0:T(128)}, u32[]{:S(2)}) copy-start(s32[128]{0:T(128)} %param.16) | copy-start | bytes 1540
  2.9 34.5 %all-to-all-start = ((bf16[32,8,1536]{2,0,1:T(8,128)(2,1)}), bf16[32,8,1536]{2,0,1:T(8,128)(2,1)S(1)}, u32[]{:S(2)}, u32[]{:S(2)}) async-start(bf16[32,8,1536]{2,0,1:T(8,128)(2,1)} %pad_maximum_fusion), calls=%async_computation | async-start | bytes 1572864 | tf_op jit(solution)/shard_map/all_to_all | solution.py:204
  37.4 0.8 collective-permute-start
  38.2 2.7 %collective-permute-start.1 = (bf16[1,128,256]{2,1,0:T(8,128)(2,1)S(1)}, bf16[1,128,256]{2,1,0:T(8,128)(2,1)S(1)}, u32[]{:S(2)}, u32[]{:S(2)}) collective-permute-start(bf16[1,128,256]{2,1,0:T(8,128)(2,1)S(1)} %broadcast_select_fusion.2), channel_id=1, source_target_pairs={{0,16},{8,24},{1,17},{9,25},{2,18},{10,26},{3,19},{11,27},{4,20},{... | collective-permute-start | bytes 196616 | tf_op jit(solution)/shard_map/ppermute | solution.py:38
  38.8 7.9 %collective-permute-start.2 = (bf16[1,128,256]{2,1,0:T(8,128)(2,1)S(1)}, bf16[1,128,256]{2,1,0:T(8,128)(2,1)S(1)}, u32[]{:S(2)}, u32[]{:S(2)}) collective-permute-start(bf16[1,128,256]{2,1,0:T(8,128)(2,1)S(1)} %broadcast_select_fusion.2), channel_id=1, source_target_pairs={{0,32},{8,40},{1,33},{9,41},{2,34},{10,42},{3,35},{11,43},{4,36},{... | collective-permute-start | bytes 196616 | tf_op jit(solution)/shard_map/ppermute | solution.py:38
  40.1 6.6 %collective-permute-start.3 = (bf16[1,128,256]{2,1,0:T(8,128)(2,1)S(1)}, bf16[1,128,256]{2,1,0:T(8,128)(2,1)S(1)}, u32[]{:S(2)}, u32[]{:S(2)}) collective-permute-start(bf16[1,128,256]{2,1,0:T(8,128)(2,1)S(1)} %broadcast_select_fusion.2), channel_id=1, source_target_pairs={{0,48},{8,56},{1,49},{9,57},{2,50},{10,58},{3,51},{11,59},{4,52},{... | collective-permute-start | bytes 196616 | tf_op jit(solution)/shard_map/ppermute | solution.py:38
  46.7 7.4 %collective-permute-start.10 = (bf16[1,128,256]{2,1,0:T(8,128)(2,1)S(1)}, bf16[1,128,256]{2,1,0:T(8,128)(2,1)S(1)}, u32[]{:S(2)}, u32[]{:S(2)}) collective-permute-start(bf16[1,128,256]{2,1,0:T(8,128)(2,1)S(1)} %add_select_fusion.1), channel_id=1, source_target_pairs={{0,448},{8,456},{16,464},{24,472},{32,480},{40,488},{48,496},{56,5... | collective-permute-start | bytes 196616 | tf_op jit(solution)/shard_map/ppermute | solution.py:38
  48.0 7.4 %collective-permute-start.4 = (bf16[1,128,256]{2,1,0:T(8,128)(2,1)S(1)}, bf16[1,128,256]{2,1,0:T(8,128)(2,1)S(1)}, u32[]{:S(2)}, u32[]{:S(2)}) collective-permute-start(bf16[1,128,256]{2,1,0:T(8,128)(2,1)S(1)} %add_select_fusion.1), channel_id=1, source_target_pairs={{0,64},{8,72},{16,80},{24,88},{32,96},{40,104},{48,112},{56,120},{... | collective-permute-start | bytes 196616 | tf_op jit(solution)/shard_map/ppermute | solution.py:38
  50.2 6.5 %collective-permute-start.5 = (bf16[1,128,256]{2,1,0:T(8,128)(2,1)S(1)}, bf16[1,128,256]{2,1,0:T(8,128)(2,1)S(1)}, u32[]{:S(2)}, u32[]{:S(2)}) collective-permute-start(bf16[1,128,256]{2,1,0:T(8,128)(2,1)S(1)} %add_select_fusion.1), channel_id=1, source_target_pairs={{0,128},{8,136},{16,144},{24,152},{32,160},{40,168},{48,176},{56,1... | collective-permute-start | bytes 196616 | tf_op jit(solution)/shard_map/ppermute | solution.py:38
  51.5 9.6 %collective-permute-start.6 = (bf16[1,128,256]{2,1,0:T(8,128)(2,1)S(1)}, bf16[1,128,256]{2,1,0:T(8,128)(2,1)S(1)}, u32[]{:S(2)}, u32[]{:S(2)}) collective-permute-start(bf16[1,128,256]{2,1,0:T(8,128)(2,1)S(1)} %add_select_fusion.1), channel_id=1, source_target_pairs={{0,192},{8,200},{16,208},{24,216},{32,224},{40,232},{48,240},{56,2... | collective-permute-start | bytes 196616 | tf_op jit(solution)/shard_map/ppermute | solution.py:38
  52.8 10.2 %collective-permute-start.7 = (bf16[1,128,256]{2,1,0:T(8,128)(2,1)S(1)}, bf16[1,128,256]{2,1,0:T(8,128)(2,1)S(1)}, u32[]{:S(2)}, u32[]{:S(2)}) collective-permute-start(bf16[1,128,256]{2,1,0:T(8,128)(2,1)S(1)} %add_select_fusion.1), channel_id=1, source_target_pairs={{0,256},{8,264},{16,272},{24,280},{32,288},{40,296},{48,304},{56,3... | collective-permute-start | bytes 196616 | tf_op jit(solution)/shard_map/ppermute | solution.py:38
  54.1 8.9 %collective-permute-start.8 = (bf16[1,128,256]{2,1,0:T(8,128)(2,1)S(1)}, bf16[1,128,256]{2,1,0:T(8,128)(2,1)S(1)}, u32[]{:S(2)}, u32[]{:S(2)}) collective-permute-start(bf16[1,128,256]{2,1,0:T(8,128)(2,1)S(1)} %add_select_fusion.1), channel_id=1, source_target_pairs={{0,320},{8,328},{16,336},{24,344},{32,352},{40,360},{48,368},{56,3... | collective-permute-start | bytes 196616 | tf_op jit(solution)/shard_map/ppermute | solution.py:38
  55.5 7.6 %collective-permute-start.9 = (bf16[1,128,256]{2,1,0:T(8,128)(2,1)S(1)}, bf16[1,128,256]{2,1,0:T(8,128)(2,1)S(1)}, u32[]{:S(2)}, u32[]{:S(2)}) collective-permute-start(bf16[1,128,256]{2,1,0:T(8,128)(2,1)S(1)} %add_select_fusion.1), channel_id=1, source_target_pairs={{0,384},{8,392},{16,400},{24,408},{32,416},{40,424},{48,432},{56,4... | collective-permute-start | bytes 196616 | tf_op jit(solution)/shard_map/ppermute | solution.py:38
  56.8 6.9 %collective-permute-start.11 = (bf16[2,128,256]{2,1,0:T(8,128)(2,1)S(1)}, bf16[2,128,256]{2,1,0:T(8,128)(2,1)S(1)}, u32[]{:S(2)}, u32[]{:S(2)}) collective-permute-start(bf16[2,128,256]{2,1,0:T(8,128)(2,1)S(1)} %pad_maximum_fusion.3), channel_id=1, source_target_pairs={{0,16},{8,24},{16,32},{24,40},{32,48},{40,56},{48,64},{56,72},{64,... | collective-permute-start | bytes 393224 | tf_op jit(solution)/shard_map/ppermute | solution.py:76
  61.1 6.3 %collective-permute-start.12 = (bf16[2,128,256]{2,1,0:T(8,128)(2,1)S(1)}, bf16[2,128,256]{2,1,0:T(8,128)(2,1)S(1)}, u32[]{:S(2)}, u32[]{:S(2)}) collective-permute-start(bf16[2,128,256]{2,1,0:T(8,128)(2,1)S(1)} %pad_maximum_fusion.3), channel_id=1, source_target_pairs={{0,8},{8,16},{16,24},{24,32},{32,40},{40,48},{48,56},{56,64},{64,7... | collective-permute-start | bytes 393224 | tf_op jit(solution)/shard_map/ppermute | solution.py:76
  80.6 1.5 copy-start.2
  82.2 10.8 %collective-permute-start.15 = (f32[1,128,256]{2,1,0:T(8,128)S(1)}, f32[1,128,256]{2,1,0:T(8,128)S(1)}, u32[]{:S(2)}, u32[]{:S(2)}) collective-permute-start(f32[1,128,256]{2,1,0:T(8,128)S(1)} %fusion.6), channel_id=1, source_target_pairs={{256,0},{264,8},{272,16},{280,24},{288,32},{296,40},{304,48},{312,... | collective-permute-start | bytes 393224 | tf_op jit(solution)/shard_map/ppermute | solution.py:65
  93.0 9.2 %collective-permute-start.16 = (f32[1,128,256]{2,1,0:T(8,128)S(1)}, f32[1,128,256]{2,1,0:T(8,128)S(1)}, u32[]{:S(2)}, u32[]{:S(2)}) collective-permute-start(f32[1,128,256]{2,1,0:T(8,128)S(1)} %add.106), channel_id=1, source_target_pairs={{128,0},{136,8},{144,16},{152,24},{160,32},{168,40},{176,48},{184,... | collective-permute-start | bytes 393224 | tf_op jit(solution)/shard_map/ppermute | solution.py:65
  102.2 6.9 %collective-permute-start.17 = (f32[1,128,256]{2,1,0:T(8,128)S(1)}, f32[1,128,256]{2,1,0:T(8,128)S(1)}, u32[]{:S(2)}, u32[]{:S(2)}) collective-permute-start(f32[1,128,256]{2,1,0:T(8,128)S(1)} %add.107), channel_id=1, source_target_pairs={{64,0},{72,8},{80,16},{88,24},{96,32},{104,40},{112,48},{120,56},{... | collective-permute-start | bytes 393224 | tf_op jit(solution)/shard_map/ppermute | solution.py:65
  109.1 8.0 %collective-permute-start.18 = (f32[1,128,256]{2,1,0:T(8,128)S(1)}, f32[1,128,256]{2,1,0:T(8,128)S(1)}, u32[]{:S(2)}, u32[]{:S(2)}) collective-permute-start(f32[1,128,256]{2,1,0:T(8,128)S(1)} %add.108), channel_id=1, source_target_pairs={{16,0},{24,8},{17,1},{25,9},{18,2},{26,10},{19,3},{27,11},{20,4},{... | collective-permute-start | bytes 393224 | tf_op jit(solution)/shard_map/ppermute | solution.py:65
  109.7 7.3 %collective-permute-start.19 = (f32[1,128,256]{2,1,0:T(8,128)S(1)}, f32[1,128,256]{2,1,0:T(8,128)S(1)}, u32[]{:S(2)}, u32[]{:S(2)}) collective-permute-start(f32[1,128,256]{2,1,0:T(8,128)S(1)} %add.108), channel_id=1, source_target_pairs={{32,0},{40,8},{33,1},{41,9},{34,2},{42,10},{35,3},{43,11},{36,4},{... | collective-permute-start | bytes 393224 | tf_op jit(solution)/shard_map/ppermute | solution.py:65
  111.0 6.0 %collective-permute-start.20 = (f32[1,128,256]{2,1,0:T(8,128)S(1)}, f32[1,128,256]{2,1,0:T(8,128)S(1)}, u32[]{:S(2)}, u32[]{:S(2)}) collective-permute-start(f32[1,128,256]{2,1,0:T(8,128)S(1)} %add.108), channel_id=1, source_target_pairs={{48,0},{56,8},{49,1},{57,9},{50,2},{58,10},{51,3},{59,11},{52,4},{... | collective-permute-start | bytes 393224 | tf_op jit(solution)/shard_map/ppermute | solution.py:65
  112.0 7.4 %collective-permute-start.13 = (f32[2,128,256]{2,1,0:T(8,128)S(1)}, f32[2,128,256]{2,1,0:T(8,128)S(1)}, u32[]{:S(2)}, u32[]{:S(2)}) collective-permute-start(f32[2,128,256]{2,1,0:T(8,128)S(1)} %bitcast.110), channel_id=1, source_target_pairs={{8,0},{16,8},{24,16},{32,24},{40,32},{48,40},{56,48},{64,56},{72,6... | collective-permute-start | bytes 786440 | tf_op jit(solution)/shard_map/ppermute | solution.py:76
  114.0 12.0 %collective-permute-start.14 = (f32[2,128,256]{2,1,0:T(8,128)S(1)}, f32[2,128,256]{2,1,0:T(8,128)S(1)}, u32[]{:S(2)}, u32[]{:S(2)}) collective-permute-start(f32[2,128,256]{2,1,0:T(8,128)S(1)} %bitcast.111), channel_id=1, source_target_pairs={{16,0},{24,8},{32,16},{40,24},{48,32},{56,40},{64,48},{72,56},{80,... | collective-permute-start | bytes 786440 | tf_op jit(solution)/shard_map/ppermute | solution.py:76
  117.1 9.0 %copy-start.3 = (bf16[256,640]{1,0:T(8,128)(2,1)S(1)}, bf16[256,640]{1,0:T(8,128)(2,1)}, u32[]{:S(2)}) copy-start(bf16[256,640]{1,0:T(8,128)(2,1)} %get-tuple-element.20) | copy-start | bytes 983044
  117.1 8.9 %collective-permute-start.21 = (f32[1,128,256]{2,1,0:T(8,128)S(1)}, f32[1,128,256]{2,1,0:T(8,128)S(1)}, u32[]{:S(2)}, u32[]{:S(2)}) collective-permute-start(f32[1,128,256]{2,1,0:T(8,128)S(1)} %add_add_fusion), channel_id=1, source_target_pairs={{8,0},{9,1},{10,2},{11,3},{12,4},{13,5},{14,6},{15,7}} | collective-permute-start | bytes 393224 | tf_op jit(solution)/shard_map/ppermute | solution.py:65
